TPU v7x, 512 devices: a whole 4x8x8 slice. The times are simulated.
512 devices in a mesh: tile: 128 (over z, y, core), freq: 4 (over x).
Axes of the slice: x: 4, y: 8, z: 8, core: 2. Of those that a mesh axis runs over, the one named last changes fastest.
Arguments:
- observed: float32 [4, 4096, 128], P('freq', 'tile'), may hold values from -6 to 6
- factor_u: float32 [2, 4, 4096, 4096], P(None, 'freq', 'tile'), may hold values from -0.03125 to 0.03125
- factor_v: float32 [2, 4, 16384, 1024], P(None, 'freq', 'tile'), may hold values from -0.125 to 0.125
- tile_ranks: int32 [4, 16, 64], P('freq'), may hold values from 16 to 64
Outputs:
- estimate: float32 [16384, 1024], P('tile', 'freq')
- residual: float32 [4, 4096, 128], P('freq', 'tile')
Inputs may be any that keep to these rules, and one draw needn't show every extreme that they name: Columns r >= tile_ranks[f, i, j] of tile (i, j)'s factors are padding and do not enter the kernel.
All inputs are finite; a program needn't handle non-finite values.
Results may differ from a plain program's by a relative error of at most 0.0001.
Values sent between devices are 32-bit elements; how exact they have to be, the bound alone decides.
No kernel may reach another device: no remote copies, remote signals or barrier semaphores. Data moves between devices by JAX's collectives and lax.ppermute only.
A program may use at most 64 MiB of HBM per device.

v0:
```python
import math

import jax
import jax.numpy as jnp
from jax import lax
from jax.sharding import PartitionSpec as P

R = 64
TIMES = 16

step_size = 0.25
shrink_factor = 0.5
energy_floor = 1e-06
matmul_precision = lax.Precision.HIGH


def contract(form, left, right):
    return jnp.einsum(form, left, right, precision=matmul_precision)


def phases(freq_index, time_index, total_times):
    turn_count = (2 * freq_index[:, None] + 1) * time_index[None, :] % total_times
    angle_rad = turn_count.astype(jnp.float32) * (2.0 * math.pi / total_times)
    weight = 1.0 / math.sqrt(total_times)
    return (jnp.cos(angle_rad) * weight, jnp.sin(angle_rad) * weight)


def local(observed, factor_u, factor_v, tile_ranks):
    tile_count = lax.axis_size("tile")
    freq_count = lax.axis_size("freq")
    position = lax.axis_index("tile")
    freq_pos = lax.axis_index("freq")
    core = position % 2
    column = position // 2
    rows_u = factor_u.shape[2]
    rows_v = factor_v.shape[2]
    row_tiles = factor_v.shape[3] // R
    col_tiles = factor_u.shape[3] // R
    sources = observed.shape[2] // 2
    half = sources // 2
    quarter = half // 2
    chips_per_row_tile = tile_count // row_tiles // 2
    times_here = TIMES // freq_count
    total_times = times_here * freq_count
    entries = rows_v * tile_count * total_times * sources
    chunk = (quarter, 2 * R)

    pair = [(k, k ^ 1) for k in range(tile_count)]

    def swap(x):
        return lax.ppermute(x, "tile", pair)

    u_own = factor_u[:, 0]
    v_own = factor_v[:, 0]
    obs_own = observed[0]
    u_both = jnp.concatenate([u_own, swap(u_own)], axis=1)
    v_both = jnp.concatenate([v_own, swap(v_own)], axis=1)
    obs_both = jnp.concatenate([obs_own, swap(obs_own)], axis=0)
    obs_split = obs_both.reshape(2 * rows_u, 2, 2, half)
    target = lax.dynamic_index_in_dim(obs_split, core, axis=2, keepdims=False).transpose(2, 1, 0)

    def weights(f_both, rows, tiles):
        split = f_both.reshape(2, rows, tiles, R).transpose(2, 0, 1, 3)
        real, imag = split[:, 0], split[:, 1]
        left = jnp.concatenate([real, imag], axis=1)
        right = jnp.concatenate([-imag, real], axis=1)
        return jnp.concatenate([left, right], axis=2)

    w_u = weights(u_both, 2 * rows_u, col_tiles)
    w_v = weights(v_both, 2 * rows_v, row_tiles)

    rank_column = lax.dynamic_index_in_dim(tile_ranks[0], column, axis=1, keepdims=False)
    rank_mask = (jnp.arange(R, dtype=jnp.int32)[None, :] < rank_column[:, None]).astype(jnp.float32)
    rank_mask = jnp.concatenate([rank_mask, rank_mask], axis=1)

    all_freqs = jnp.arange(freq_count, dtype=jnp.int32)
    all_times = jnp.arange(total_times, dtype=jnp.int32)
    cos_tab, sin_tab = phases(all_freqs, all_times, total_times)

    def adjoint(resid):
        lhs = resid.reshape(half, 2 * 2 * rows_u)
        e = contract("vq,jqo->jvo", lhs, w_u)
        outgoing = e.reshape((tile_count,) + chunk)
        incoming = lax.all_to_all(outgoing, "tile", 0, 0, tiled=True)
        gathered = incoming.reshape((row_tiles, chips_per_row_tile, 2) + chunk).sum(axis=1)
        gathered = gathered.reshape(row_tiles, half, 2 * R) * rank_mask[:, None, :]
        blocks = contract("ivo,iqo->ivq", gathered, w_v).sum(axis=0)
        return blocks.reshape(half, 2, 2 * rows_v)

    def all_freq(spectrum):
        outgoing = jnp.broadcast_to(spectrum[None], (freq_count,) + spectrum.shape)
        return lax.all_to_all(outgoing, "freq", 0, 0, tiled=True)

    def to_time(spectra):
        total = 0.0
        for f in range(freq_count):
            total = total + (
                cos_tab[f][:, None, None] * spectra[f, :, 0][None]
                - sin_tab[f][:, None, None] * spectra[f, :, 1][None]
            )
        return total

    def threshold_of(update):
        energy = jnp.sum(update * update)
        outgoing = jnp.broadcast_to(energy, (tile_count, 1))
        total = jnp.sum(lax.all_to_all(outgoing, "tile", 0, 0, tiled=True))
        return shrink_factor * jnp.sqrt(total / entries + energy_floor)

    grad1 = adjoint(target)
    update1 = step_size * to_time(all_freq(grad1))
    threshold1 = threshold_of(update1)
    first = update1 - jnp.clip(update1, -threshold1, threshold1)

    cos_q = lax.dynamic_index_in_dim(cos_tab, freq_pos, axis=0, keepdims=False)
    sin_q = lax.dynamic_index_in_dim(sin_tab, freq_pos, axis=0, keepdims=False)
    x_re = jnp.sum(cos_q[:, None, None] * first, axis=0)
    x_im = -jnp.sum(sin_q[:, None, None] * first, axis=0)
    lhs = jnp.stack([x_re, x_im], axis=1).reshape(half, 2 * 2 * rows_v)
    coeffs = contract("vq,iqo->ivo", lhs, w_v) * rank_mask[:, None, :]
    outgoing = jnp.broadcast_to(
        coeffs.reshape((row_tiles, 1, 2) + chunk),
        (row_tiles, chips_per_row_tile, 2) + chunk,
    ).reshape((tile_count,) + chunk)
    incoming = lax.all_to_all(outgoing, "tile", 0, 0, tiled=True)
    summed = incoming.reshape(col_tiles, half, 2 * R)
    y = contract("jvo,jqo->jvq", summed, w_u).sum(axis=0)
    residual = y.reshape(half, 2, 2 * rows_u) - target

    grad2 = adjoint(residual)
    update2 = first - step_size * to_time(all_freq(grad2))
    threshold2 = threshold_of(update2)
    mine = lax.dynamic_slice_in_dim(update2, freq_pos * times_here, times_here, axis=0)
    mine = mine - jnp.clip(mine, -threshold2, threshold2)
    mine = mine.reshape(times_here, 2, quarter, 2, rows_v)
    own = mine[:, :, :, 0]
    other = swap(mine[:, :, :, 1])
    first_b = jnp.where(core == 0, own, other)
    second_b = jnp.where(core == 0, other, own)
    estimate = jnp.stack([first_b, second_b], axis=2).transpose(4, 0, 1, 2, 3)
    estimate = estimate.reshape(rows_v, times_here * sources)

    res_own = residual[:, :, :rows_u]
    res_other = swap(residual[:, :, rows_u:])
    lo = jnp.where(core == 0, res_own, res_other)
    hi = jnp.where(core == 0, res_other, res_own)
    residual_out = jnp.stack([lo, hi]).transpose(3, 2, 0, 1).reshape(1, rows_u, 2 * sources)
    return (estimate, residual_out)


def solution(mesh):
    placed = (
        P("freq", "tile", None),
        P(None, "freq", "tile", None),
        P(None, "freq", "tile", None),
        P("freq", None, None),
    )
    return jax.shard_map(
        local,
        mesh=mesh,
        in_specs=placed,
        out_specs=(P("tile", "freq"), P("freq", "tile", None)),
        check_vma=False,
    )
```

profile of v0, /device:TPU:1, one launch (start us, length us, event | category | flops | bytes accessed | tf_op | source)
XLA Modules:
  0.0 238.0 jit_solution(8451223834990476743)
XLA Ops:
  0.7 8.9 %collective-permute-start = (f32[2,32,4096]{2,1,0:T(8,128)}, f32[2,32,4096]{2,1,0:T(8,128)}, u32[]{:S(2)}, u32[]{:S(2)}) collective-permute-start(f32[2,32,4096]{2,1,0:T(8,128)} %bitcast.175), channel_id=1, source_target_pairs={{0,4},{4,0},{8,12},{12,8},{16,20},{20,16},{24,28},{28,24},{32,36},... | collective-permute-start | bytes 3145736 | tf_op jit(solution)/shard_map/ppermute | solution.py:51
  9.6 1.9 collective-permute-start.1
  11.5 1.5 copy.54
  13.1 2.4 %collective-permute-start.2 = (f32[2,128,1024]{1,2,0:T(8,128)S(1)}, f32[2,128,1024]{1,2,0:T(8,128)}, u32[]{:S(2)}, u32[]{:S(2)}) collective-permute-start(f32[2,128,1024]{1,2,0:T(8,128)S(1)} %bitcast.169), channel_id=1, source_target_pairs={{0,4},{4,0},{8,12},{12,8},{16,20},{20,16},{24,28},{28,24},{32,36},... | collective-permute-start | bytes 3145736 | tf_op jit(solution)/shard_map/ppermute | solution.py:51
  15.5 2.0 concatenate.48
  17.6 2.6 %copy.49 = f32[2,32,64,64]{3,1,2,0:T(8,128)} copy(f32[2,32,64,64]{3,2,1,0:T(8,128)S(1)} %concatenate.48) | data formatting | bytes 2097152 | tf_op jit(solution)/shard_map/concatenate | solution.py:56
  20.7 2.0 concatenate.49
  22.7 1.2 copy.50
  24.0 0.4 copy-done.3
  24.3 0.6 maximum_bitcast_fusion
  25.4 1.1 maximum_maximum_fusion
  26.6 1.9 copy-done.1
  28.5 2.2 fusion.13
  30.7 12.1 %all-to-all-start = ((f32[128,16,128]{2,1,0:T(8,128)}), f32[128,16,128]{2,1,0:T(8,128)}, u32[]{:S(2)}, u32[]{:S(2)}) async-start(f32[128,16,128]{2,1,0:T(8,128)} %bitcast.9), calls=%async_computation | async-start | bytes 2097152 | tf_op jit(solution)/shard_map/all_to_all | solution.py:84
  42.8 0.6 copy.56
  44.0 3.2 %copy.57 = f32[2,128,16,64]{3,1,2,0:T(8,128)} copy(f32[2,128,16,64]{1,3,2,0:T(8,128)} %bitcast.16) | data formatting | bytes 2097152 | tf_op jit(solution)/shard_map/concatenate | solution.py:57
  47.1 1.9 maximum_bitcast_fusion.1
  49.5 3.1 %maximum_maximum_fusion.1 = f32[16,512,128]{2,1,0:T(8,128)} fusion(f32[16,256,64]{2,1,0:T(8,128)S(1)} %get-tuple-element.13, f32[16,256,64]{2,1,0:T(8,128)S(1)} %fusion.11, f32[16,256,64]{2,1,0:T(8,128)S(1)} %get-tuple-element.12), kind=kLoop, calls=%fused_computation.3 | loop fusion | flops 3145728 | bytes 7340032 | tf_op jit(solution)/shard_map/concatenate | solution.py:67
  52.6 20.7 %all-to-all-done = f32[128,16,128]{2,1,0:T(8,128)} async-done(((f32[128,16,128]{2,1,0:T(8,128)}), f32[128,16,128]{2,1,0:T(8,128)}, u32[]{:S(2)}, u32[]{:S(2)}) %all-to-all-start) | async-done | bytes 1048608 | tf_op jit(solution)/shard_map/all_to_all | solution.py:84
  73.4 1.3 reduce_sum.70
  74.7 4.1 %convolution_bitcast_fusion.1 = f32[32,2,256]{2,0,1:T(8,128)S(1)} fusion(f32[2,256,128,16]{2,1,0,3:T(8,128)} %bitcast.167, f32[16,32,128]{2,1,0:T(8,128)S(1)} %bitcast_multiply_fusion.1), kind=kOutput, calls=%fused_computation.10 | convolution fusion | flops 201326592 | bytes 4521984 | tf_op jit(solution)/shard_map/ivo,iqo->ivq/dot_general | solution.py:18
  78.9 0.7 broadcast_in_dim.12
  79.6 4.0 %all-to-all-start.1 = ((f32[4,32,2,256]{3,1,2,0:T(8,128)}), f32[4,32,2,256]{3,1,2,0:T(8,128)S(1)}, u32[]{:S(2)}, u32[]{:S(2)}) async-start(f32[4,32,2,256]{3,1,2,0:T(8,128)} %broadcast_in_dim.12), calls=%async_computation.1 | async-start | bytes 524288 | tf_op jit(solution)/shard_map/all_to_all | solution.py:92
  83.6 5.9 %all-to-all-done.1 = f32[4,32,2,256]{3,1,2,0:T(8,128)S(1)} async-done(((f32[4,32,2,256]{3,1,2,0:T(8,128)}), f32[4,32,2,256]{3,1,2,0:T(8,128)S(1)}, u32[]{:S(2)}, u32[]{:S(2)}) %all-to-all-start.1) | async-done | bytes 262176 | tf_op jit(solution)/shard_map/all_to_all | solution.py:92
  89.5 1.1 multiply_reduce_fusion.3
  90.6 0.7 broadcast_in_dim.13
  91.3 18.8 %all_to_all.37 = f32[128,1,1]{2,1,0:T(1,128)S(1)} all-to-all(f32[128,1,1]{2,1,0:T(1,128)S(1)} %broadcast_in_dim.13), channel_id=1, replica_groups=mesh['tile'=128,'freq'=4] {'tile'}, dimensions={0} | all-to-all | bytes 1024 | tf_op jit(solution)/shard_map/all_to_all | solution.py:106
  110.2 0.7 reduce_sum.72
  111.6 0.5 multiply_reduce_fusion.1
  112.1 0.5 multiply_reduce_fusion.2
  112.8 3.5 %convolution_multiply_fusion = f32[16,128,32]{1,2,0:T(8,128)S(1)} fusion(f32[16,512,128]{2,1,0:T(8,128)} %maximum_maximum_fusion.1, f32[32,512,1]{1,0,2:T(8,128)S(1)} %reshape.143, f32[16,128]{1,0:T(8,128)S(1)} %add_convert_fusion), kind=kOutput, calls=%fused_computation.8 | convolution fusion | flops 201392128 | bytes 4530176 | tf_op jit(solution)/shard_map/vq,iqo->ivo/dot_general | solution.py:18
  116.5 36.1 %all_to_all.38 = f32[128,16,128]{2,1,0:T(8,128)S(1)} all-to-all(f32[128,16,128]{2,1,0:T(8,128)S(1)} %bitcast.172), channel_id=1, replica_groups=mesh['tile'=128,'freq'=4] {'tile'}, dimensions={0} | all-to-all | bytes 2097152 | tf_op jit(solution)/shard_map/all_to_all | solution.py:124
  152.6 2.9 %fusion = f32[32,2,64]{2,0,1:T(8,128)S(1)} fusion(f32[32,2,64]{2,0,1:T(8,128)S(1)} %fusion.4, f32[64,32,128,1]{2,1,3,0:T(8,128)S(1)} %bitcast.174, f32[2,64,128,64]{2,1,0,3:T(8,128)S(1)} %bitcast.166), kind=kOutput, calls=%fused_computation.12 | convolution fusion | flops 201330688 | bytes 5275648 | tf_op jit(solution)/shard_map/jvo,jqo->jvq/dot_general | solution.py:18
  155.7 3.2 %fusion.14 = f32[64,128,32]{1,2,0:T(8,128)S(1)} fusion(f32[64,128,128]{2,1,0:T(8,128)} %copy-done.1, f32[32,128,1]{1,0,2:T(8,128)S(1)} %reshape.146), kind=kOutput, calls=%fused_computation.80 | convolution fusion | flops 201326592 | bytes 5259264 | tf_op jit(solution)/shard_map/vq,jqo->jvo/dot_general | solution.py:18
  158.9 37.2 %all_to_all.39 = f32[128,16,128]{2,1,0:T(8,128)S(1)} all-to-all(f32[128,16,128]{2,1,0:T(8,128)S(1)} %bitcast.171), channel_id=1, replica_groups=mesh['tile'=128,'freq'=4] {'tile'}, dimensions={0} | all-to-all | bytes 2097152 | tf_op jit(solution)/shard_map/all_to_all | solution.py:84
  196.2 4.1 %convolution_bitcast_fusion = f32[32,2,256]{2,0,1:T(8,128)S(1)} fusion(f32[2,256,128,16]{2,1,0,3:T(8,128)} %bitcast.168, f32[16,32,128]{2,1,0:T(8,128)S(1)} %bitcast_multiply_fusion), kind=kOutput, calls=%fused_computation.9 | convolution fusion | flops 201326592 | bytes 4521984 | tf_op jit(solution)/shard_map/ivo,iqo->ivq/dot_general | solution.py:18
  200.3 0.7 broadcast_in_dim.16
  201.1 3.4 %all-to-all-start.5 = ((f32[4,32,2,256]{3,1,2,0:T(8,128)}), f32[4,32,2,256]{3,1,2,0:T(8,128)S(1)}, u32[]{:S(2)}, u32[]{:S(2)}) async-start(f32[4,32,2,256]{3,1,2,0:T(8,128)} %broadcast_in_dim.16), calls=%async_computation.5 | async-start | bytes 524288 | tf_op jit(solution)/shard_map/all_to_all | solution.py:92
  204.5 2.2 collective-permute-start.4
  206.7 3.9 %all-to-all-done.5 = f32[4,32,2,256]{3,1,2,0:T(8,128)S(1)} async-done(((f32[4,32,2,256]{3,1,2,0:T(8,128)}), f32[4,32,2,256]{3,1,2,0:T(8,128)S(1)}, u32[]{:S(2)}, u32[]{:S(2)}) %all-to-all-start.5) | async-done | bytes 262176 | tf_op jit(solution)/shard_map/all_to_all | solution.py:92
  210.7 1.5 multiply_reduce_fusion
  212.2 1.3 broadcast_in_dim.17
  213.5 7.3 %all-to-all-start.6 = ((f32[128,1,1]{2,1,0:T(1,128)}), f32[128,1,1]{2,1,0:T(1,128)S(1)}, u32[]{:S(2)}, u32[]{:S(2)}) async-start(f32[128,1,1]{2,1,0:T(1,128)} %broadcast_in_dim.17), calls=%async_computation.6 | async-start | bytes 131072 | tf_op jit(solution)/shard_map/all_to_all | solution.py:106
  220.8 11.4 %all-to-all-done.6 = f32[128,1,1]{2,1,0:T(1,128)S(1)} async-done(((f32[128,1,1]{2,1,0:T(1,128)}), f32[128,1,1]{2,1,0:T(1,128)S(1)}, u32[]{:S(2)}, u32[]{:S(2)}) %all-to-all-start.6) | async-done | bytes 544 | tf_op jit(solution)/shard_map/all_to_all | solution.py:106
  232.2 0.7 reduce_sum.91
  233.8 2.5 %collective-permute-start.3 = (f32[4,2,16,128]{3,2,1,0:T(8,128)S(1)}, f32[4,2,16,128]{3,2,1,0:T(8,128)S(1)}, u32[]{:S(2)}, u32[]{:S(2)}) collective-permute-start(f32[4,2,16,128]{3,2,1,0:T(8,128)S(1)} %bitcast.179), channel_id=1, source_target_pairs={{0,4},{4,0},{8,12},{12,8},{16,20},{20,16},{24,28},{28,24},{32,36},... | collective-permute-start | bytes 196616 | tf_op jit(solution)/shard_map/ppermute | solution.py:51
  236.4 0.7 reshape.139
  237.2 0.8 copy.68
  (53 shorter events, 3.1 us)
Async XLA Ops:
  0.6 42.8 %copy-start = (s32[1,16,64]{2,1,0:T(8,128)S(1)}, s32[1,16,64]{2,1,0:T(8,128)}, u32[]{:S(2)}) copy-start(s32[1,16,64]{2,1,0:T(8,128)} %param.7) | copy-start | bytes 12292
  0.6 16.9 %copy-start.4 = (f32[1,32,128]{2,1,0:T(8,128)S(1)}, f32[1,32,128]{2,1,0:T(8,128)}, u32[]{:S(2)}) copy-start(f32[1,32,128]{2,1,0:T(8,128)} %param.4) | copy-start | bytes 49156
  0.7 20.1 %collective-permute-start = (f32[2,32,4096]{2,1,0:T(8,128)}, f32[2,32,4096]{2,1,0:T(8,128)}, u32[]{:S(2)}, u32[]{:S(2)}) collective-permute-start(f32[2,32,4096]{2,1,0:T(8,128)} %bitcast.175), channel_id=1, source_target_pairs={{0,4},{4,0},{8,12},{12,8},{16,20},{20,16},{24,28},{28,24},{32,36},... | collective-permute-start | bytes 3145736 | tf_op jit(solution)/shard_map/ppermute | solution.py:51
  9.6 10.7 %collective-permute-start.1 = (f32[32,128]{1,0:T(8,128)}, f32[32,128]{1,0:T(8,128)S(1)}, u32[]{:S(2)}, u32[]{:S(2)}) collective-permute-start(f32[32,128]{1,0:T(8,128)} %bitcast.180), channel_id=1, source_target_pairs={{0,4},{4,0},{8,12},{12,8},{16,20},{20,16},{24,28},{28,24},{32,36},... | collective-permute-start | bytes 49160 | tf_op jit(solution)/shard_map/ppermute | solution.py:51
  13.1 30.9 %collective-permute-start.2 = (f32[2,128,1024]{1,2,0:T(8,128)S(1)}, f32[2,128,1024]{1,2,0:T(8,128)}, u32[]{:S(2)}, u32[]{:S(2)}) collective-permute-start(f32[2,128,1024]{1,2,0:T(8,128)S(1)} %bitcast.169), channel_id=1, source_target_pairs={{0,4},{4,0},{8,12},{12,8},{16,20},{20,16},{24,28},{28,24},{32,36},... | collective-permute-start | bytes 3145736 | tf_op jit(solution)/shard_map/ppermute | solution.py:51
  22.7 1.6 copy-start.3
  26.6 1.9 copy-start.1
  30.7 42.7 %all-to-all-start = ((f32[128,16,128]{2,1,0:T(8,128)}), f32[128,16,128]{2,1,0:T(8,128)}, u32[]{:S(2)}, u32[]{:S(2)}) async-start(f32[128,16,128]{2,1,0:T(8,128)} %bitcast.9), calls=%async_computation | async-start | bytes 2097152 | tf_op jit(solution)/shard_map/all_to_all | solution.py:84
  79.6 9.9 %all-to-all-start.1 = ((f32[4,32,2,256]{3,1,2,0:T(8,128)}), f32[4,32,2,256]{3,1,2,0:T(8,128)S(1)}, u32[]{:S(2)}, u32[]{:S(2)}) async-start(f32[4,32,2,256]{3,1,2,0:T(8,128)} %broadcast_in_dim.12), calls=%async_computation.1 | async-start | bytes 524288 | tf_op jit(solution)/shard_map/all_to_all | solution.py:92
  112.8 39.8 %copy-start.2 = (f32[64,128,128]{2,1,0:T(8,128)S(1)}, f32[64,128,128]{2,1,0:T(8,128)}, u32[]{:S(2)}) copy-start(f32[64,128,128]{2,1,0:T(8,128)} %copy-done.1) | copy-start | bytes 12582916
  201.1 9.6 %all-to-all-start.5 = ((f32[4,32,2,256]{3,1,2,0:T(8,128)}), f32[4,32,2,256]{3,1,2,0:T(8,128)S(1)}, u32[]{:S(2)}, u32[]{:S(2)}) async-start(f32[4,32,2,256]{3,1,2,0:T(8,128)} %broadcast_in_dim.16), calls=%async_computation.5 | async-start | bytes 524288 | tf_op jit(solution)/shard_map/all_to_all | solution.py:92
  204.5 16.2 %collective-permute-start.4 = (f32[32,2,32]{2,0,1:T(8,128)S(1)}, f32[32,2,32]{2,0,1:T(8,128)S(1)}, u32[]{:S(2)}, u32[]{:S(2)}) collective-permute-start(f32[32,2,32]{2,0,1:T(8,128)S(1)} %slice.175), channel_id=1, source_target_pairs={{0,4},{4,0},{8,12},{12,8},{16,20},{20,16},{24,28},{28,24},{32,36},... | collective-permute-start | bytes 24584 | tf_op jit(solution)/shard_map/ppermute | solution.py:51
  213.5 18.7 %all-to-all-start.6 = ((f32[128,1,1]{2,1,0:T(1,128)}), f32[128,1,1]{2,1,0:T(1,128)S(1)}, u32[]{:S(2)}, u32[]{:S(2)}) async-start(f32[128,1,1]{2,1,0:T(1,128)} %broadcast_in_dim.17), calls=%async_computation.6 | async-start | bytes 131072 | tf_op jit(solution)/shard_map/all_to_all | solution.py:106
  233.8 3.4 %collective-permute-start.3 = (f32[4,2,16,128]{3,2,1,0:T(8,128)S(1)}, f32[4,2,16,128]{3,2,1,0:T(8,128)S(1)}, u32[]{:S(2)}, u32[]{:S(2)}) collective-permute-start(f32[4,2,16,128]{3,2,1,0:T(8,128)S(1)} %bitcast.179), channel_id=1, source_target_pairs={{0,4},{4,0},{8,12},{12,8},{16,20},{20,16},{24,28},{28,24},{32,36},... | collective-permute-start | bytes 196616 | tf_op jit(solution)/shard_map/ppermute | solution.py:51
where the time goes:
time: 239 us; the launch traced here: 238 us
  blocking collectives  92.2 us (39%)
  starting transfers between devices  44.7 us (19%)
  waiting for transfers between devices  42 us (18%)
  local copies, waits for them, and re-layouts  22.3 us (9%)
  matrix products  20.1 us (8%)
  other arithmetic  14.2 us (6%)
  between operations  2.58 us (1%)
    all_to_all x1, blocking collectives, adjoint(): incoming = lax.all_to_all(outgoing, 'tile', 0, 0, tiled=True)  37.2 us
    all_to_all x1, blocking collectives, local(): incoming = lax.all_to_all(outgoing, 'tile', 0, 0, tiled=True)  36.1 us
    all_to_all x1, waiting for transfers between devices, adjoint(): incoming = lax.all_to_all(outgoing, 'tile', 0, 0, tiled=True)  20.7 us
    dot_general x6, matrix products, contract(): return jnp.einsum(form, left, right, precision=matmul_precision)  20.1 us
    all_to_all x1, blocking collectives, threshold_of(): total = jnp.sum(lax.all_to_all(outgoing, 'tile', 0, 0, tiled=True))  18.8 us
    ppermute x5, starting transfers between devices, swap(): return lax.ppermute(x, 'tile', pair)  17.9 us
    all_to_all x1, starting transfers between devices, adjoint(): incoming = lax.all_to_all(outgoing, 'tile', 0, 0, tiled=True)  12.1 us
    all_to_all x1, waiting for transfers between devices, threshold_of(): total = jnp.sum(lax.all_to_all(outgoing, 'tile', 0, 0, tiled=True))  11.4 us
  transfers between devices with their start and end apart: 9, of which 4 were waited for; matrix products, arithmetic and copies ran while one was open for 12% of the time, Pallas kernels for 0%

commit v1 on v0

--- a/solution.py
+++ b/solution.py
@@ -53,7 +53,9 @@
     u_own = factor_u[:, 0]
     v_own = factor_v[:, 0]
     obs_own = observed[0]
-    u_both = jnp.concatenate([u_own, swap(u_own)], axis=1)
+    u_other = swap(u_own)
+    u_both = jnp.concatenate([u_own, u_other], axis=1)
+    v_own, _ = lax.optimization_barrier((v_own, u_other))
     v_both = jnp.concatenate([v_own, swap(v_own)], axis=1)
     obs_both = jnp.concatenate([obs_own, swap(obs_own)], axis=0)
     obs_split = obs_both.reshape(2 * rows_u, 2, 2, half)

time: 239 us -> 238 us (level)
    concatenate x6 -> x4, local copies, waits for them, and re-layouts: 11.5 us -> 6.61 us  [local(): u_both = jnp.concatenate([u_own, u_other], axis=1)]
    reshape x0 -> x1, local copies, waits for them, and re-layouts: none -> 2.73 us  [weights(): split = f_both.reshape(2, rows, tiles, R).transpose(2, 0, 1, 3)]
  transfers between devices with their start and end apart: 9 -> 9, of which waited for: 4 -> 4; matrix products, arithmetic and copies ran while one was open for 12% -> 11% of each run, Pallas kernels for 0% -> 0%
where the time goes in v1:
time: 238 us; the launch traced here: 237 us
  blocking collectives  92.2 us (39%)
  starting transfers between devices  44.1 us (19%)
  waiting for transfers between devices  40.8 us (17%)
  local copies, waits for them, and re-layouts  22.9 us (10%)
  matrix products  20.1 us (8%)
  other arithmetic  14.4 us (6%)
  between operations  2.54 us (1%)
    all_to_all x1, blocking collectives, adjoint(): incoming = lax.all_to_all(outgoing, 'tile', 0, 0, tiled=True)  37.2 us
    all_to_all x1, blocking collectives, local(): incoming = lax.all_to_all(outgoing, 'tile', 0, 0, tiled=True)  36.1 us
    dot_general x6, matrix products, contract(): return jnp.einsum(form, left, right, precision=matmul_precision)  20.1 us
    all_to_all x1, waiting for transfers between devices, adjoint(): incoming = lax.all_to_all(outgoing, 'tile', 0, 0, tiled=True)  19.6 us
    all_to_all x1, blocking collectives, threshold_of(): total = jnp.sum(lax.all_to_all(outgoing, 'tile', 0, 0, tiled=True))  18.9 us
    ppermute x5, starting transfers between devices, swap(): return lax.ppermute(x, 'tile', pair)  17.8 us
    all_to_all x1, starting transfers between devices, adjoint(): incoming = lax.all_to_all(outgoing, 'tile', 0, 0, tiled=True)  11.7 us
    all_to_all x1, waiting for transfers between devices, threshold_of(): total = jnp.sum(lax.all_to_all(outgoing, 'tile', 0, 0, tiled=True))  11.4 us
  transfers between devices with their start and end apart: 9, of which 4 were waited for; matrix products, arithmetic and copies ran while one was open for 11% of the time, Pallas kernels for 0%

profile of v1, /device:TPU:1, one launch (start us, length us, event | category | flops | bytes accessed | tf_op | source)
XLA Modules:
  0.0 237.1 jit_solution(2878618037299444211)
XLA Ops:
  0.6 8.8 %collective-permute-start = (f32[2,32,4096]{2,1,0:T(8,128)}, f32[2,32,4096]{2,1,0:T(8,128)S(1)}, u32[]{:S(2)}, u32[]{:S(2)}) collective-permute-start(f32[2,32,4096]{2,1,0:T(8,128)} %bitcast.175), channel_id=1, source_target_pairs={{0,4},{4,0},{8,12},{12,8},{16,20},{20,16},{24,28},{28,24},{32,36},... | collective-permute-start | bytes 3145736 | tf_op jit(solution)/shard_map/ppermute | solution.py:51
  9.4 1.9 collective-permute-start.1
  11.4 2.0 concatenate.43
  13.4 0.8 concatenate.49
  14.2 2.5 %copy.50 = f32[2,1,128,1024]{2,3,0,1:T(8,128)} copy(f32[2,1,128,1024]{3,2,1,0:T(8,128)} %param.6) | data formatting | bytes 2097152 | tf_op args[2]
  16.8 2.6 %copy.45 = f32[2,32,64,64]{3,1,2,0:T(8,128)} copy(f32[2,32,64,64]{3,2,1,0:T(8,128)S(1)} %concatenate.43) | data formatting | bytes 2097152 | tf_op jit(solution)/shard_map/concatenate | solution.py:57
  19.8 0.8 concatenate.44
  20.7 1.2 copy.46
  22.3 0.6 maximum_bitcast_fusion
  23.4 2.4 %collective-permute-start.2 = (f32[2,128,1024]{1,2,0:T(8,128)}, f32[2,128,1024]{1,2,0:T(8,128)}, u32[]{:S(2)}, u32[]{:S(2)}) collective-permute-start(f32[2,128,1024]{1,2,0:T(8,128)} %bitcast.14), channel_id=1, source_target_pairs={{0,4},{4,0},{8,12},{12,8},{16,20},{20,16},{24,28},{28,24},{32,36},... | collective-permute-start | bytes 3145736 | tf_op jit(solution)/shard_map/ppermute | solution.py:51
  25.8 1.1 maximum_maximum_fusion
  27.0 1.9 copy-done.1
  28.9 2.2 fusion.13
  31.1 11.7 %all-to-all-start = ((f32[128,16,128]{2,1,0:T(8,128)}), f32[128,16,128]{2,1,0:T(8,128)S(1)}, u32[]{:S(2)}, u32[]{:S(2)}) async-start(f32[128,16,128]{2,1,0:T(8,128)} %bitcast.9), calls=%async_computation | async-start | bytes 2097152 | tf_op jit(solution)/shard_map/all_to_all | solution.py:86
  43.3 1.7 pad_maximum_fusion
  45.0 2.7 %copy.51 = f32[2,256,16,64]{3,1,2,0:T(8,128)} copy(f32[2,256,16,64]{1,3,2,0:T(8,128)S(1)} %bitcast.169) | data formatting | bytes 4194304 | tf_op jit(solution)/shard_map/reshape | solution.py:65
  47.7 1.9 fusion.11
  49.7 0.9 copy-done.3
  51.0 3.1 %maximum_maximum_fusion.1 = f32[16,512,128]{2,1,0:T(8,128)} fusion(f32[16,256,64]{2,1,0:T(8,128)S(1)} %get-tuple-element.15, f32[16,256,64]{2,1,0:T(8,128)S(1)} %fusion.11, f32[16,256,64]{2,1,0:T(8,128)S(1)} %get-tuple-element.14), kind=kLoop, calls=%fused_computation.2 | loop fusion | flops 3145728 | bytes 7340032 | tf_op jit(solution)/shard_map/concatenate | solution.py:69
  54.1 19.6 %all-to-all-done = f32[128,16,128]{2,1,0:T(8,128)S(1)} async-done(((f32[128,16,128]{2,1,0:T(8,128)}), f32[128,16,128]{2,1,0:T(8,128)S(1)}, u32[]{:S(2)}, u32[]{:S(2)}) %all-to-all-start) | async-done | bytes 1048608 | tf_op jit(solution)/shard_map/all_to_all | solution.py:86
  73.9 4.1 %convolution_bitcast_fusion.1 = f32[32,2,256]{2,0,1:T(8,128)S(1)} fusion(f32[2,256,128,16]{2,1,0,3:T(8,128)} %bitcast.165, f32[16,32,128]{2,1,0:T(8,128)S(1)} %bitcast_multiply_fusion.1), kind=kOutput, calls=%fused_computation.10 | convolution fusion | flops 201326592 | bytes 4521984 | tf_op jit(solution)/shard_map/ivo,iqo->ivq/dot_general | solution.py:18
  78.0 0.7 broadcast_in_dim.12
  78.7 4.0 %all-to-all-start.1 = ((f32[4,32,2,256]{3,1,2,0:T(8,128)}), f32[4,32,2,256]{3,1,2,0:T(8,128)S(1)}, u32[]{:S(2)}, u32[]{:S(2)}) async-start(f32[4,32,2,256]{3,1,2,0:T(8,128)} %broadcast_in_dim.12), calls=%async_computation.1 | async-start | bytes 524288 | tf_op jit(solution)/shard_map/all_to_all | solution.py:94
  82.7 5.9 %all-to-all-done.1 = f32[4,32,2,256]{3,1,2,0:T(8,128)S(1)} async-done(((f32[4,32,2,256]{3,1,2,0:T(8,128)}), f32[4,32,2,256]{3,1,2,0:T(8,128)S(1)}, u32[]{:S(2)}, u32[]{:S(2)}) %all-to-all-start.1) | async-done | bytes 262176 | tf_op jit(solution)/shard_map/all_to_all | solution.py:94
  88.6 1.1 multiply_reduce_fusion.3
  89.7 0.7 broadcast_in_dim.13
  90.4 18.9 %all_to_all.37 = f32[128,1,1]{2,1,0:T(1,128)S(1)} all-to-all(f32[128,1,1]{2,1,0:T(1,128)S(1)} %broadcast_in_dim.13), channel_id=1, replica_groups=mesh['tile'=128,'freq'=4] {'tile'}, dimensions={0} | all-to-all | bytes 1024 | tf_op jit(solution)/shard_map/all_to_all | solution.py:108
  109.3 0.7 reduce_sum.72
  110.7 0.5 multiply_reduce_fusion.1
  111.2 0.5 multiply_reduce_fusion.2
  111.9 3.5 %convolution_multiply_fusion = f32[16,128,32]{1,2,0:T(8,128)S(1)} fusion(f32[16,512,128]{2,1,0:T(8,128)} %maximum_maximum_fusion.1, f32[32,512,1]{1,0,2:T(8,128)S(1)} %reshape.143, f32[16,128]{1,0:T(8,128)S(1)} %add_convert_fusion), kind=kOutput, calls=%fused_computation.8 | convolution fusion | flops 201392128 | bytes 4530176 | tf_op jit(solution)/shard_map/vq,iqo->ivo/dot_general | solution.py:18
  115.6 36.1 %all_to_all.38 = f32[128,16,128]{2,1,0:T(8,128)S(1)} all-to-all(f32[128,16,128]{2,1,0:T(8,128)S(1)} %bitcast.171), channel_id=1, replica_groups=mesh['tile'=128,'freq'=4] {'tile'}, dimensions={0} | all-to-all | bytes 2097152 | tf_op jit(solution)/shard_map/all_to_all | solution.py:126
  151.7 2.9 %fusion = f32[32,2,64]{2,0,1:T(8,128)S(1)} fusion(f32[32,2,64]{2,0,1:T(8,128)S(1)} %fusion.4, f32[64,32,128,1]{2,1,3,0:T(8,128)S(1)} %bitcast.174, f32[2,64,128,64]{2,1,0,3:T(8,128)S(1)} %bitcast.164), kind=kOutput, calls=%fused_computation.12 | convolution fusion | flops 201330688 | bytes 5275648 | tf_op jit(solution)/shard_map/jvo,jqo->jvq/dot_general | solution.py:18
  154.8 3.2 %fusion.14 = f32[64,128,32]{1,2,0:T(8,128)S(1)} fusion(f32[64,128,128]{2,1,0:T(8,128)} %copy-done.1, f32[32,128,1]{1,0,2:T(8,128)S(1)} %reshape.146), kind=kOutput, calls=%fused_computation.80 | convolution fusion | flops 201326592 | bytes 5259264 | tf_op jit(solution)/shard_map/vq,jqo->jvo/dot_general | solution.py:18
  158.0 37.2 %all_to_all.39 = f32[128,16,128]{2,1,0:T(8,128)S(1)} all-to-all(f32[128,16,128]{2,1,0:T(8,128)S(1)} %bitcast.170), channel_id=1, replica_groups=mesh['tile'=128,'freq'=4] {'tile'}, dimensions={0} | all-to-all | bytes 2097152 | tf_op jit(solution)/shard_map/all_to_all | solution.py:86
  195.3 4.1 %convolution_bitcast_fusion = f32[32,2,256]{2,0,1:T(8,128)S(1)} fusion(f32[2,256,128,16]{2,1,0,3:T(8,128)} %bitcast.166, f32[16,32,128]{2,1,0:T(8,128)S(1)} %bitcast_multiply_fusion), kind=kOutput, calls=%fused_computation.9 | convolution fusion | flops 201326592 | bytes 4521984 | tf_op jit(solution)/shard_map/ivo,iqo->ivq/dot_general | solution.py:18
  199.4 0.7 broadcast_in_dim.16
  200.2 3.4 %all-to-all-start.5 = ((f32[4,32,2,256]{3,1,2,0:T(8,128)}), f32[4,32,2,256]{3,1,2,0:T(8,128)S(1)}, u32[]{:S(2)}, u32[]{:S(2)}) async-start(f32[4,32,2,256]{3,1,2,0:T(8,128)} %broadcast_in_dim.16), calls=%async_computation.5 | async-start | bytes 524288 | tf_op jit(solution)/shard_map/all_to_all | solution.py:94
  203.7 2.2 collective-permute-start.4
  205.8 3.9 %all-to-all-done.5 = f32[4,32,2,256]{3,1,2,0:T(8,128)S(1)} async-done(((f32[4,32,2,256]{3,1,2,0:T(8,128)}), f32[4,32,2,256]{3,1,2,0:T(8,128)S(1)}, u32[]{:S(2)}, u32[]{:S(2)}) %all-to-all-start.5) | async-done | bytes 262176 | tf_op jit(solution)/shard_map/all_to_all | solution.py:94
  209.8 1.5 multiply_reduce_fusion
  211.3 1.3 broadcast_in_dim.17
  212.6 7.3 %all-to-all-start.6 = ((f32[128,1,1]{2,1,0:T(1,128)}), f32[128,1,1]{2,1,0:T(1,128)S(1)}, u32[]{:S(2)}, u32[]{:S(2)}) async-start(f32[128,1,1]{2,1,0:T(1,128)} %broadcast_in_dim.17), calls=%async_computation.6 | async-start | bytes 131072 | tf_op jit(solution)/shard_map/all_to_all | solution.py:108
  219.9 11.4 %all-to-all-done.6 = f32[128,1,1]{2,1,0:T(1,128)S(1)} async-done(((f32[128,1,1]{2,1,0:T(1,128)}), f32[128,1,1]{2,1,0:T(1,128)S(1)}, u32[]{:S(2)}, u32[]{:S(2)}) %all-to-all-start.6) | async-done | bytes 544 | tf_op jit(solution)/shard_map/all_to_all | solution.py:108
  231.3 0.7 reduce_sum.91
  232.9 2.5 %collective-permute-start.3 = (f32[4,2,16,128]{3,2,1,0:T(8,128)S(1)}, f32[4,2,16,128]{3,2,1,0:T(8,128)S(1)}, u32[]{:S(2)}, u32[]{:S(2)}) collective-permute-start(f32[4,2,16,128]{3,2,1,0:T(8,128)S(1)} %bitcast.179), channel_id=1, source_target_pairs={{0,4},{4,0},{8,12},{12,8},{16,20},{20,16},{24,28},{28,24},{32,36},... | collective-permute-start | bytes 196616 | tf_op jit(solution)/shard_map/ppermute | solution.py:51
  235.5 0.7 reshape.139
  236.4 0.8 copy.62
  (52 shorter events, 3.4 us)
Async XLA Ops:
  0.6 42.2 %copy-start = (s32[1,16,64]{2,1,0:T(8,128)S(1)}, s32[1,16,64]{2,1,0:T(8,128)}, u32[]{:S(2)}) copy-start(s32[1,16,64]{2,1,0:T(8,128)} %param.7) | copy-start | bytes 12292
  0.6 19.2 %collective-permute-start = (f32[2,32,4096]{2,1,0:T(8,128)}, f32[2,32,4096]{2,1,0:T(8,128)S(1)}, u32[]{:S(2)}, u32[]{:S(2)}) collective-permute-start(f32[2,32,4096]{2,1,0:T(8,128)} %bitcast.175), channel_id=1, source_target_pairs={{0,4},{4,0},{8,12},{12,8},{16,20},{20,16},{24,28},{28,24},{32,36},... | collective-permute-start | bytes 3145736 | tf_op jit(solution)/shard_map/ppermute | solution.py:51
  9.4 10.0 %collective-permute-start.1 = (f32[32,128]{1,0:T(8,128)}, f32[32,128]{1,0:T(8,128)S(1)}, u32[]{:S(2)}, u32[]{:S(2)}) collective-permute-start(f32[32,128]{1,0:T(8,128)} %bitcast.180), channel_id=1, source_target_pairs={{0,4},{4,0},{8,12},{12,8},{16,20},{20,16},{24,28},{28,24},{32,36},... | collective-permute-start | bytes 49160 | tf_op jit(solution)/shard_map/ppermute | solution.py:51
  20.7 1.6 copy-start.4
  23.4 19.9 %collective-permute-start.2 = (f32[2,128,1024]{1,2,0:T(8,128)}, f32[2,128,1024]{1,2,0:T(8,128)}, u32[]{:S(2)}, u32[]{:S(2)}) collective-permute-start(f32[2,128,1024]{1,2,0:T(8,128)} %bitcast.14), channel_id=1, source_target_pairs={{0,4},{4,0},{8,12},{12,8},{16,20},{20,16},{24,28},{28,24},{32,36},... | collective-permute-start | bytes 3145736 | tf_op jit(solution)/shard_map/ppermute | solution.py:51
  27.0 1.9 copy-start.1
  31.1 42.6 %all-to-all-start = ((f32[128,16,128]{2,1,0:T(8,128)}), f32[128,16,128]{2,1,0:T(8,128)S(1)}, u32[]{:S(2)}, u32[]{:S(2)}) async-start(f32[128,16,128]{2,1,0:T(8,128)} %bitcast.9), calls=%async_computation | async-start | bytes 2097152 | tf_op jit(solution)/shard_map/all_to_all | solution.py:86
  47.7 2.8 %copy-start.3 = (f32[2,256,16,64]{3,1,2,0:T(8,128)S(1)}, f32[2,256,16,64]{3,1,2,0:T(8,128)}, u32[]{:S(2)}) copy-start(f32[2,256,16,64]{3,1,2,0:T(8,128)} %copy.51) | copy-start | bytes 6291460
  78.7 9.9 %all-to-all-start.1 = ((f32[4,32,2,256]{3,1,2,0:T(8,128)}), f32[4,32,2,256]{3,1,2,0:T(8,128)S(1)}, u32[]{:S(2)}, u32[]{:S(2)}) async-start(f32[4,32,2,256]{3,1,2,0:T(8,128)} %broadcast_in_dim.12), calls=%async_computation.1 | async-start | bytes 524288 | tf_op jit(solution)/shard_map/all_to_all | solution.py:94
  111.9 39.8 %copy-start.2 = (f32[64,128,128]{2,1,0:T(8,128)S(1)}, f32[64,128,128]{2,1,0:T(8,128)}, u32[]{:S(2)}) copy-start(f32[64,128,128]{2,1,0:T(8,128)} %copy-done.1) | copy-start | bytes 12582916
  200.2 9.6 %all-to-all-start.5 = ((f32[4,32,2,256]{3,1,2,0:T(8,128)}), f32[4,32,2,256]{3,1,2,0:T(8,128)S(1)}, u32[]{:S(2)}, u32[]{:S(2)}) async-start(f32[4,32,2,256]{3,1,2,0:T(8,128)} %broadcast_in_dim.16), calls=%async_computation.5 | async-start | bytes 524288 | tf_op jit(solution)/shard_map/all_to_all | solution.py:94
  203.7 16.2 %collective-permute-start.4 = (f32[32,2,32]{2,0,1:T(8,128)S(1)}, f32[32,2,32]{2,0,1:T(8,128)S(1)}, u32[]{:S(2)}, u32[]{:S(2)}) collective-permute-start(f32[32,2,32]{2,0,1:T(8,128)S(1)} %slice.175), channel_id=1, source_target_pairs={{0,4},{4,0},{8,12},{12,8},{16,20},{20,16},{24,28},{28,24},{32,36},... | collective-permute-start | bytes 24584 | tf_op jit(solution)/shard_map/ppermute | solution.py:51
  212.6 18.7 %all-to-all-start.6 = ((f32[128,1,1]{2,1,0:T(1,128)}), f32[128,1,1]{2,1,0:T(1,128)S(1)}, u32[]{:S(2)}, u32[]{:S(2)}) async-start(f32[128,1,1]{2,1,0:T(1,128)} %broadcast_in_dim.17), calls=%async_computation.6 | async-start | bytes 131072 | tf_op jit(solution)/shard_map/all_to_all | solution.py:108
  232.9 3.4 %collective-permute-start.3 = (f32[4,2,16,128]{3,2,1,0:T(8,128)S(1)}, f32[4,2,16,128]{3,2,1,0:T(8,128)S(1)}, u32[]{:S(2)}, u32[]{:S(2)}) collective-permute-start(f32[4,2,16,128]{3,2,1,0:T(8,128)S(1)} %bitcast.179), channel_id=1, source_target_pairs={{0,4},{4,0},{8,12},{12,8},{16,20},{20,16},{24,28},{28,24},{32,36},... | collective-permute-start | bytes 196616 | tf_op jit(solution)/shard_map/ppermute | solution.py:51

commit v2 on v1

--- a/solution.py
+++ b/solution.py
@@ -3,6 +3,7 @@
 import jax
 import jax.numpy as jnp
 from jax import lax
+from jax.experimental import pallas as pl
 from jax.sharding import PartitionSpec as P
 
 R = 64
@@ -23,6 +24,31 @@
     angle_rad = turn_count.astype(jnp.float32) * (2.0 * math.pi / total_times)
     weight = 1.0 / math.sqrt(total_times)
     return (jnp.cos(angle_rad) * weight, jnp.sin(angle_rad) * weight)
+
+
+def weight_kernel(own_ref, other_ref, out_ref):
+    for jj in range(2):
+        lo, hi = jj * R, (jj + 1) * R
+        re = jnp.concatenate([own_ref[0, :, lo:hi], other_ref[0, :, lo:hi]], axis=0)
+        im = jnp.concatenate([own_ref[1, :, lo:hi], other_ref[1, :, lo:hi]], axis=0)
+        rows = re.shape[0]
+        out_ref[jj, :rows, :R] = re
+        out_ref[jj, rows:, :R] = im
+        out_ref[jj, :rows, R:] = -im
+        out_ref[jj, rows:, R:] = re
+
+
+def build_weights(own, other):
+    rows, cols = own.shape[1], own.shape[2]
+    tiles = cols // R
+    spec = pl.BlockSpec((2, rows, 2 * R), lambda p: (0, 0, p))
+    return pl.pallas_call(
+        weight_kernel,
+        grid=(tiles // 2,),
+        in_specs=[spec, spec],
+        out_specs=pl.BlockSpec((2, 4 * rows, 2 * R), lambda p: (p, 0, 0)),
+        out_shape=jax.ShapeDtypeStruct((tiles, 4 * rows, 2 * R), own.dtype),
+    )(own, other)
 
 
 def local(observed, factor_u, factor_v, tile_ranks):
@@ -54,22 +80,14 @@
     v_own = factor_v[:, 0]
     obs_own = observed[0]
     u_other = swap(u_own)
-    u_both = jnp.concatenate([u_own, u_other], axis=1)
     v_own, _ = lax.optimization_barrier((v_own, u_other))
-    v_both = jnp.concatenate([v_own, swap(v_own)], axis=1)
+    v_other = swap(v_own)
     obs_both = jnp.concatenate([obs_own, swap(obs_own)], axis=0)
     obs_split = obs_both.reshape(2 * rows_u, 2, 2, half)
     target = lax.dynamic_index_in_dim(obs_split, core, axis=2, keepdims=False).transpose(2, 1, 0)
 
-    def weights(f_both, rows, tiles):
-        split = f_both.reshape(2, rows, tiles, R).transpose(2, 0, 1, 3)
-        real, imag = split[:, 0], split[:, 1]
-        left = jnp.concatenate([real, imag], axis=1)
-        right = jnp.concatenate([-imag, real], axis=1)
-        return jnp.concatenate([left, right], axis=2)
-
-    w_u = weights(u_both, 2 * rows_u, col_tiles)
-    w_v = weights(v_both, 2 * rows_v, row_tiles)
+    w_u = build_weights(u_own, u_other)
+    w_v = build_weights(v_own, v_other)
 
     rank_column = lax.dynamic_index_in_dim(tile_ranks[0], column, axis=1, keepdims=False)
     rank_mask = (jnp.arange(R, dtype=jnp.int32)[None, :] < rank_column[:, None]).astype(jnp.float32)

time: 238 us -> 245 us (1.029)
  Pallas kernels: 0 us -> 24.1 us
  local copies, waits for them, and re-layouts: 22.9 us -> 9.01 us
  other arithmetic: 14.4 us -> 5.78 us
    pallas_call x0 -> x2, Pallas kernels: none -> 24.1 us  [build_weights(): pl.pallas_call(weight_kernel, grid=(tiles // 2,), in_specs=[spec, spec],...]
    concatenate x4 -> x0, local copies, waits for them, and re-layouts: 6.61 us -> none  [local(): u_both = jnp.concatenate([u_own, u_other], axis=1)]
    concatenate x3 -> x0, other arithmetic: 5.94 us -> none  [the longest x2 4.26 us: weights(): return jnp.concatenate([left, right], axis=2)]
    unnamed x12 -> x11, local copies, waits for them, and re-layouts: 6.48 us -> 2.72 us
    reshape x1 -> x0, local copies, waits for them, and re-layouts: 2.73 us -> none  [weights(): split = f_both.reshape(2, rows, tiles, R).transpose(2, 0, 1, 3)]
  transfers between devices with their start and end apart: 9 -> 9, of which waited for: 4 -> 6; matrix products, arithmetic and copies ran while one was open for 11% -> 2% of each run, Pallas kernels for 0% -> 3%
where the time goes in v2:
time: 245 us; the launch traced here: 242 us
  blocking collectives  92.3 us (38%)
  starting transfers between devices  44.6 us (18%)
  waiting for transfers between devices  41.3 us (17%)
  Pallas kernels  24.1 us (10%)
  matrix products  22.3 us (9%)
  local copies, waits for them, and re-layouts  9.01 us (4%)
  other arithmetic  5.78 us (2%)
  between operations  2.45 us (1%)
    all_to_all x1, blocking collectives, adjoint(): incoming = lax.all_to_all(outgoing, 'tile', 0, 0, tiled=True)  37.2 us
    all_to_all x1, blocking collectives, local(): incoming = lax.all_to_all(outgoing, 'tile', 0, 0, tiled=True)  36.3 us
    pallas_call x2, Pallas kernels, build_weights(): pl.pallas_call(weight_kernel, grid=(tiles // 2,), in_specs=[spec, spec],...  24.1 us
    dot_general x6, matrix products, contract(): return jnp.einsum(form, left, right, precision=matmul_precision)  22.3 us
    all_to_all x1, blocking collectives, threshold_of(): total = jnp.sum(lax.all_to_all(outgoing, 'tile', 0, 0, tiled=True))  18.8 us
    ppermute x5, starting transfers between devices, swap(): return lax.ppermute(x, 'tile', pair)  18.2 us
    all_to_all x1, waiting for transfers between devices, adjoint(): incoming = lax.all_to_all(outgoing, 'tile', 0, 0, tiled=True)  17.9 us
    all_to_all x1, starting transfers between devices, adjoint(): incoming = lax.all_to_all(outgoing, 'tile', 0, 0, tiled=True)  11.7 us
  transfers between devices with their start and end apart: 9, of which 6 were waited for; matrix products, arithmetic and copies ran while one was open for 2% of the time, Pallas kernels for 3%

profile of v2, /device:TPU:1, one launch (start us, length us, event | category | flops | bytes accessed | tf_op | source)
XLA Modules:
  0.0 241.9 jit_solution(9119113642442611037)
XLA Ops:
  0.6 8.8 %collective-permute-start = (f32[2,32,4096]{2,1,0:T(8,128)}, f32[2,32,4096]{2,1,0:T(8,128)S(1)}, u32[]{:S(2)}, u32[]{:S(2)}) collective-permute-start(f32[2,32,4096]{2,1,0:T(8,128)} %bitcast.153), channel_id=1, source_target_pairs={{0,4},{4,0},{8,12},{12,8},{16,20},{20,16},{24,28},{28,24},{32,36},... | collective-permute-start | bytes 3145736 | tf_op jit(solution)/shard_map/ppermute | solution.py:77
  9.4 1.9 collective-permute-start.1
  11.4 0.8 concatenate.14
  12.3 0.4 collective-permute-done.1
  12.7 0.1 concatenate.15
  13.1 1.0 copy-done.3
  14.1 17.2 %shard_map.59 = f32[64,128,128]{2,1,0:T(8,128)} custom-call(f32[2,32,4096]{2,1,0:T(8,128)} %bitcast.154, f32[2,32,4096]{2,1,0:T(8,128)} %copy-done.3), custom_call_target="tpu_custom_call" | custom-call | tf_op jit(solution)/shard_map/pallas_call | solution.py:45
  31.3 4.4 %fusion.11 = f32[64,128,32]{1,2,0:T(8,128)} fusion(f32[64,128,128]{2,1,0:T(8,128)} %shard_map.59, f32[32,128,1]{1,0,2:T(8,128)S(1)} %reshape.132), kind=kOutput, calls=%fused_computation.69 | convolution fusion | flops 201326592 | bytes 5259264 | tf_op jit(solution)/shard_map/vq,jqo->jvo/dot_general | solution.py:19
  35.7 11.7 %all-to-all-start = ((f32[128,16,128]{2,1,0:T(8,128)}), f32[128,16,128]{2,1,0:T(8,128)S(1)}, u32[]{:S(2)}, u32[]{:S(2)}) async-start(f32[128,16,128]{2,1,0:T(8,128)} %bitcast.6), calls=%async_computation | async-start | bytes 2097152 | tf_op jit(solution)/shard_map/all_to_all | solution.py:104
  47.4 2.8 %collective-permute-start.2 = (f32[2,128,1024]{2,1,0:T(8,128)S(1)}, f32[2,128,1024]{2,1,0:T(8,128)S(1)}, u32[]{:S(2)}, u32[]{:S(2)}) collective-permute-start(f32[2,128,1024]{2,1,0:T(8,128)S(1)} %bitcast.156), channel_id=1, source_target_pairs={{0,4},{4,0},{8,12},{12,8},{16,20},{20,16},{24,28},{28,24},{32,36},... | collective-permute-start | bytes 3145736 | tf_op jit(solution)/shard_map/ppermute | solution.py:77
  50.2 0.2 dynamic-slice_reduce_fusion
  50.6 0.1 cosine_multiply_fusion
  50.7 1.8 collective-permute-done.2.other_ref
  52.5 1.0 copy-done.4
  53.5 6.9 %shard_map.60 = f32[16,512,128]{2,1,0:T(8,128)} custom-call(f32[2,128,1024]{2,1,0:T(8,128)} %bitcast.155, f32[2,128,1024]{2,1,0:T(8,128)} %copy-done.4), custom_call_target="tpu_custom_call" | custom-call | tf_op jit(solution)/shard_map/pallas_call | solution.py:45
  60.4 17.9 %all-to-all-done = f32[128,16,128]{2,1,0:T(8,128)S(1)} async-done(((f32[128,16,128]{2,1,0:T(8,128)}), f32[128,16,128]{2,1,0:T(8,128)S(1)}, u32[]{:S(2)}, u32[]{:S(2)}) %all-to-all-start) | async-done | bytes 1048608 | tf_op jit(solution)/shard_map/all_to_all | solution.py:104
  78.3 0.1 reduce_sum.70
  78.4 4.1 %convolution_bitcast_fusion.1 = f32[32,2,256]{2,0,1:T(8,128)S(1)} fusion(f32[2,256,128,16]{2,1,0,3:T(8,128)} %bitcast.145, f32[16,32,128]{2,1,0:T(8,128)S(1)} %bitcast_multiply_fusion.1), kind=kOutput, calls=%fused_computation.2 | convolution fusion | flops 201326592 | bytes 4521984 | tf_op jit(solution)/shard_map/ivo,iqo->ivq/dot_general | solution.py:19
  82.5 0.7 broadcast_in_dim.12
  83.3 4.0 %all-to-all-start.1 = ((f32[4,32,2,256]{3,1,2,0:T(8,128)}), f32[4,32,2,256]{3,1,2,0:T(8,128)S(1)}, u32[]{:S(2)}, u32[]{:S(2)}) async-start(f32[4,32,2,256]{3,1,2,0:T(8,128)} %broadcast_in_dim.12), calls=%async_computation.1 | async-start | bytes 524288 | tf_op jit(solution)/shard_map/all_to_all | solution.py:112
  87.3 5.9 %all-to-all-done.1 = f32[4,32,2,256]{3,1,2,0:T(8,128)S(1)} async-done(((f32[4,32,2,256]{3,1,2,0:T(8,128)}), f32[4,32,2,256]{3,1,2,0:T(8,128)S(1)}, u32[]{:S(2)}, u32[]{:S(2)}) %all-to-all-start.1) | async-done | bytes 262176 | tf_op jit(solution)/shard_map/all_to_all | solution.py:112
  93.2 1.1 multiply_reduce_fusion.3
  94.3 0.7 broadcast_in_dim.13
  95.0 18.8 %all_to_all.37 = f32[128,1,1]{2,1,0:T(1,128)S(1)} all-to-all(f32[128,1,1]{2,1,0:T(1,128)S(1)} %broadcast_in_dim.13), channel_id=1, replica_groups=mesh['tile'=128,'freq'=4] {'tile'}, dimensions={0} | all-to-all | bytes 1024 | tf_op jit(solution)/shard_map/all_to_all | solution.py:126
  113.8 0.7 reduce_sum.72
  115.3 0.5 multiply_reduce_fusion.1
  115.8 0.5 multiply_reduce_fusion.2
  116.5 3.5 %convolution_multiply_fusion = f32[16,128,32]{1,2,0:T(8,128)S(1)} fusion(f32[16,512,128]{2,1,0:T(8,128)} %shard_map.60, f32[32,512,1]{1,0,2:T(8,128)S(1)} %reshape.135, f32[16,128]{1,0:T(8,128)S(1)} %add_convert_fusion), kind=kOutput, calls=%fused_computation | convolution fusion | flops 201392128 | bytes 4530176 | tf_op jit(solution)/shard_map/vq,iqo->ivo/dot_general | solution.py:19
  120.0 0.1 broadcast_in_dim.15
  120.1 36.3 %all_to_all.38 = f32[128,16,128]{2,1,0:T(8,128)S(1)} all-to-all(f32[128,16,128]{2,1,0:T(8,128)S(1)} %bitcast.148), channel_id=1, replica_groups=mesh['tile'=128,'freq'=4] {'tile'}, dimensions={0} | all-to-all | bytes 2097152 | tf_op jit(solution)/shard_map/all_to_all | solution.py:144
  156.5 2.9 %fusion = f32[32,2,64]{2,0,1:T(8,128)S(1)} fusion(f32[32,2,64]{2,0,1:T(8,128)S(1)} %fusion.4, f32[64,32,128,1]{2,1,3,0:T(8,128)S(1)} %bitcast.151, f32[2,64,128,64]{2,1,0,3:T(8,128)S(1)} %bitcast.144), kind=kOutput, calls=%fused_computation.4 | convolution fusion | flops 201330688 | bytes 5275648 | tf_op jit(solution)/shard_map/jvo,jqo->jvq/dot_general | solution.py:19
  159.5 3.2 %fusion.12 = f32[64,128,32]{1,2,0:T(8,128)S(1)} fusion(f32[64,128,128]{2,1,0:T(8,128)} %shard_map.59, f32[32,128,1]{1,0,2:T(8,128)S(1)} %reshape.138), kind=kOutput, calls=%fused_computation.70 | convolution fusion | flops 201326592 | bytes 5259264 | tf_op jit(solution)/shard_map/vq,jqo->jvo/dot_general | solution.py:19
  162.8 37.2 %all_to_all.39 = f32[128,16,128]{2,1,0:T(8,128)S(1)} all-to-all(f32[128,16,128]{2,1,0:T(8,128)S(1)} %bitcast.147), channel_id=1, replica_groups=mesh['tile'=128,'freq'=4] {'tile'}, dimensions={0} | all-to-all | bytes 2097152 | tf_op jit(solution)/shard_map/all_to_all | solution.py:104
  200.0 0.1 reduce_sum.89
  200.1 4.1 %convolution_bitcast_fusion = f32[32,2,256]{2,0,1:T(8,128)S(1)} fusion(f32[2,256,128,16]{2,1,0,3:T(8,128)} %bitcast.146, f32[16,32,128]{2,1,0:T(8,128)S(1)} %bitcast_multiply_fusion), kind=kOutput, calls=%fused_computation.1 | convolution fusion | flops 201326592 | bytes 4521984 | tf_op jit(solution)/shard_map/ivo,iqo->ivq/dot_general | solution.py:19
  204.2 0.7 broadcast_in_dim.16
  204.9 3.4 %all-to-all-start.5 = ((f32[4,32,2,256]{3,1,2,0:T(8,128)}), f32[4,32,2,256]{3,1,2,0:T(8,128)S(1)}, u32[]{:S(2)}, u32[]{:S(2)}) async-start(f32[4,32,2,256]{3,1,2,0:T(8,128)} %broadcast_in_dim.16), calls=%async_computation.5 | async-start | bytes 524288 | tf_op jit(solution)/shard_map/all_to_all | solution.py:112
  208.4 2.2 collective-permute-start.4
  210.6 3.9 %all-to-all-done.5 = f32[4,32,2,256]{3,1,2,0:T(8,128)S(1)} async-done(((f32[4,32,2,256]{3,1,2,0:T(8,128)}), f32[4,32,2,256]{3,1,2,0:T(8,128)S(1)}, u32[]{:S(2)}, u32[]{:S(2)}) %all-to-all-start.5) | async-done | bytes 262176 | tf_op jit(solution)/shard_map/all_to_all | solution.py:112
  214.5 1.5 multiply_reduce_fusion
  216.1 1.3 broadcast_in_dim.17
  217.4 7.3 %all-to-all-start.6 = ((f32[128,1,1]{2,1,0:T(1,128)}), f32[128,1,1]{2,1,0:T(1,128)S(1)}, u32[]{:S(2)}, u32[]{:S(2)}) async-start(f32[128,1,1]{2,1,0:T(1,128)} %broadcast_in_dim.17), calls=%async_computation.6 | async-start | bytes 131072 | tf_op jit(solution)/shard_map/all_to_all | solution.py:126
  224.7 11.4 %all-to-all-done.6 = f32[128,1,1]{2,1,0:T(1,128)S(1)} async-done(((f32[128,1,1]{2,1,0:T(1,128)}), f32[128,1,1]{2,1,0:T(1,128)S(1)}, u32[]{:S(2)}, u32[]{:S(2)}) %all-to-all-start.6) | async-done | bytes 544 | tf_op jit(solution)/shard_map/all_to_all | solution.py:126
  236.0 0.7 reduce_sum.91
  237.6 0.1 fusion.10
  237.7 2.5 %collective-permute-start.3 = (f32[4,2,16,128]{3,2,1,0:T(8,128)S(1)}, f32[4,2,16,128]{3,2,1,0:T(8,128)S(1)}, u32[]{:S(2)}, u32[]{:S(2)}) collective-permute-start(f32[4,2,16,128]{3,2,1,0:T(8,128)S(1)} %bitcast.159), channel_id=1, source_target_pairs={{0,4},{4,0},{8,12},{12,8},{16,20},{20,16},{24,28},{28,24},{32,36},... | collective-permute-start | bytes 196616 | tf_op jit(solution)/shard_map/ppermute | solution.py:77
  240.3 0.7 reshape.131
  241.1 0.8 copy.49
  (40 shorter events, 1.3 us)
Async XLA Ops:
  0.6 49.6 %copy-start = (s32[1,16,64]{2,1,0:T(8,128)S(1)}, s32[1,16,64]{2,1,0:T(8,128)}, u32[]{:S(2)}) copy-start(s32[1,16,64]{2,1,0:T(8,128)} %param.7) | copy-start | bytes 12292
  0.6 12.5 %collective-permute-start = (f32[2,32,4096]{2,1,0:T(8,128)}, f32[2,32,4096]{2,1,0:T(8,128)S(1)}, u32[]{:S(2)}, u32[]{:S(2)}) collective-permute-start(f32[2,32,4096]{2,1,0:T(8,128)} %bitcast.153), channel_id=1, source_target_pairs={{0,4},{4,0},{8,12},{12,8},{16,20},{20,16},{24,28},{28,24},{32,36},... | collective-permute-start | bytes 3145736 | tf_op jit(solution)/shard_map/ppermute | solution.py:77
  9.4 3.3 %collective-permute-start.1 = (f32[32,128]{1,0:T(8,128)}, f32[32,128]{1,0:T(8,128)S(1)}, u32[]{:S(2)}, u32[]{:S(2)}) collective-permute-start(f32[32,128]{1,0:T(8,128)} %bitcast.160), channel_id=1, source_target_pairs={{0,4},{4,0},{8,12},{12,8},{16,20},{20,16},{24,28},{28,24},{32,36},... | collective-permute-start | bytes 49160 | tf_op jit(solution)/shard_map/ppermute | solution.py:77
  13.1 1.0 copy-start.3
  31.3 16.1 %copy-start.2 = (f32[2,1,128,1024]{3,2,1,0:T(8,128)S(1)}, f32[2,1,128,1024]{3,2,1,0:T(8,128)}, u32[]{:S(2)}) copy-start(f32[2,1,128,1024]{3,2,1,0:T(8,128)} %param.6) | copy-start | bytes 3145732
  35.7 42.6 %all-to-all-start = ((f32[128,16,128]{2,1,0:T(8,128)}), f32[128,16,128]{2,1,0:T(8,128)S(1)}, u32[]{:S(2)}, u32[]{:S(2)}) async-start(f32[128,16,128]{2,1,0:T(8,128)} %bitcast.6), calls=%async_computation | async-start | bytes 2097152 | tf_op jit(solution)/shard_map/all_to_all | solution.py:104
  47.4 5.1 %collective-permute-start.2 = (f32[2,128,1024]{2,1,0:T(8,128)S(1)}, f32[2,128,1024]{2,1,0:T(8,128)S(1)}, u32[]{:S(2)}, u32[]{:S(2)}) collective-permute-start(f32[2,128,1024]{2,1,0:T(8,128)S(1)} %bitcast.156), channel_id=1, source_target_pairs={{0,4},{4,0},{8,12},{12,8},{16,20},{20,16},{24,28},{28,24},{32,36},... | collective-permute-start | bytes 3145736 | tf_op jit(solution)/shard_map/ppermute | solution.py:77
  52.5 1.0 copy-start.4
  83.3 9.9 %all-to-all-start.1 = ((f32[4,32,2,256]{3,1,2,0:T(8,128)}), f32[4,32,2,256]{3,1,2,0:T(8,128)S(1)}, u32[]{:S(2)}, u32[]{:S(2)}) async-start(f32[4,32,2,256]{3,1,2,0:T(8,128)} %broadcast_in_dim.12), calls=%async_computation.1 | async-start | bytes 524288 | tf_op jit(solution)/shard_map/all_to_all | solution.py:112
  116.5 40.0 %copy-start.1 = (f32[64,128,128]{2,1,0:T(8,128)S(1)}, f32[64,128,128]{2,1,0:T(8,128)}, u32[]{:S(2)}) copy-start(f32[64,128,128]{2,1,0:T(8,128)} %shard_map.59) | copy-start | bytes 12582916
  204.9 9.6 %all-to-all-start.5 = ((f32[4,32,2,256]{3,1,2,0:T(8,128)}), f32[4,32,2,256]{3,1,2,0:T(8,128)S(1)}, u32[]{:S(2)}, u32[]{:S(2)}) async-start(f32[4,32,2,256]{3,1,2,0:T(8,128)} %broadcast_in_dim.16), calls=%async_computation.5 | async-start | bytes 524288 | tf_op jit(solution)/shard_map/all_to_all | solution.py:112
  208.4 16.2 %collective-permute-start.4 = (f32[32,2,32]{2,0,1:T(8,128)S(1)}, f32[32,2,32]{2,0,1:T(8,128)S(1)}, u32[]{:S(2)}, u32[]{:S(2)}) collective-permute-start(f32[32,2,32]{2,0,1:T(8,128)S(1)} %slice.155), channel_id=1, source_target_pairs={{0,4},{4,0},{8,12},{12,8},{16,20},{20,16},{24,28},{28,24},{32,36},... | collective-permute-start | bytes 24584 | tf_op jit(solution)/shard_map/ppermute | solution.py:77
  217.4 18.7 %all-to-all-start.6 = ((f32[128,1,1]{2,1,0:T(1,128)}), f32[128,1,1]{2,1,0:T(1,128)S(1)}, u32[]{:S(2)}, u32[]{:S(2)}) async-start(f32[128,1,1]{2,1,0:T(1,128)} %broadcast_in_dim.17), calls=%async_computation.6 | async-start | bytes 131072 | tf_op jit(solution)/shard_map/all_to_all | solution.py:126
  237.7 3.4 %collective-permute-start.3 = (f32[4,2,16,128]{3,2,1,0:T(8,128)S(1)}, f32[4,2,16,128]{3,2,1,0:T(8,128)S(1)}, u32[]{:S(2)}, u32[]{:S(2)}) collective-permute-start(f32[4,2,16,128]{3,2,1,0:T(8,128)S(1)} %bitcast.159), channel_id=1, source_target_pairs={{0,4},{4,0},{8,12},{12,8},{16,20},{20,16},{24,28},{28,24},{32,36},... | collective-permute-start | bytes 196616 | tf_op jit(solution)/shard_map/ppermute | solution.py:77

commit v3 on v2

--- a/solution.py
+++ b/solution.py
@@ -27,7 +27,7 @@
 
 
 def weight_kernel(own_ref, other_ref, out_ref):
-    for jj in range(2):
+    for jj in range(out_ref.shape[0]):
         lo, hi = jj * R, (jj + 1) * R
         re = jnp.concatenate([own_ref[0, :, lo:hi], other_ref[0, :, lo:hi]], axis=0)
         im = jnp.concatenate([own_ref[1, :, lo:hi], other_ref[1, :, lo:hi]], axis=0)
@@ -41,15 +41,15 @@
 def build_weights(own, other):
     rows, cols = own.shape[1], own.shape[2]
     tiles = cols // R
-    spec = pl.BlockSpec((2, rows, 2 * R), lambda p: (0, 0, p))
+    per_step = min(tiles, 16)
+    spec = pl.BlockSpec((2, rows, per_step * R), lambda p: (0, 0, p))
     return pl.pallas_call(
         weight_kernel,
-        grid=(tiles // 2,),
+        grid=(tiles // per_step,),
         in_specs=[spec, spec],
-        out_specs=pl.BlockSpec((2, 4 * rows, 2 * R), lambda p: (p, 0, 0)),
+        out_specs=pl.BlockSpec((per_step, 4 * rows, 2 * R), lambda p: (p, 0, 0)),
         out_shape=jax.ShapeDtypeStruct((tiles, 4 * rows, 2 * R), own.dtype),
     )(own, other)
-
 
 def local(observed, factor_u, factor_v, tile_ranks):
     tile_count = lax.axis_size("tile")

time: 245 us -> 230 us (0.939); the launches traced: 242 us -> 229 us
  Pallas kernels: 24.1 us -> 9.41 us
    pallas_call x2, Pallas kernels: 24.1 us -> 9.41 us  [build_weights(): pl.pallas_call(weight_kernel, grid=(tiles // per_step,), in_specs=[spec,...]
  transfers between devices with their start and end apart: 9 -> 9, of which waited for: 6 -> 6; matrix products, arithmetic and copies ran while one was open for 2% -> 2% of each run, Pallas kernels for 3% -> 2%
where the time goes in v3:
time: 230 us; the launch traced here: 229 us
  blocking collectives  92.3 us (40%)
  starting transfers between devices  44.6 us (19%)
  waiting for transfers between devices  43.6 us (19%)
  matrix products  22.3 us (10%)
  Pallas kernels  9.41 us (4%)
  local copies, waits for them, and re-layouts  9.01 us (4%)
  other arithmetic  5.78 us (3%)
  between operations  2.45 us (1%)
    all_to_all x1, blocking collectives, adjoint(): incoming = lax.all_to_all(outgoing, 'tile', 0, 0, tiled=True)  37.2 us
    all_to_all x1, blocking collectives, local(): incoming = lax.all_to_all(outgoing, 'tile', 0, 0, tiled=True)  36.3 us
    dot_general x6, matrix products, contract(): return jnp.einsum(form, left, right, precision=matmul_precision)  22.3 us
    all_to_all x1, waiting for transfers between devices, adjoint(): incoming = lax.all_to_all(outgoing, 'tile', 0, 0, tiled=True)  20.2 us
    all_to_all x1, blocking collectives, threshold_of(): total = jnp.sum(lax.all_to_all(outgoing, 'tile', 0, 0, tiled=True))  18.8 us
    ppermute x5, starting transfers between devices, swap(): return lax.ppermute(x, 'tile', pair)  18.2 us
    all_to_all x1, starting transfers between devices, adjoint(): incoming = lax.all_to_all(outgoing, 'tile', 0, 0, tiled=True)  11.7 us
    all_to_all x1, waiting for transfers between devices, threshold_of(): total = jnp.sum(lax.all_to_all(outgoing, 'tile', 0, 0, tiled=True))  11.4 us
  transfers between devices with their start and end apart: 9, of which 6 were waited for; matrix products, arithmetic and copies ran while one was open for 2% of the time, Pallas kernels for 2%

profile of v3, /device:TPU:1, one launch (start us, length us, event | category | flops | bytes accessed | tf_op | source)
XLA Modules:
  0.0 229.4 jit_solution(8144426151712531073)
XLA Ops:
  0.6 8.8 %collective-permute-start = (f32[2,32,4096]{2,1,0:T(8,128)}, f32[2,32,4096]{2,1,0:T(8,128)S(1)}, u32[]{:S(2)}, u32[]{:S(2)}) collective-permute-start(f32[2,32,4096]{2,1,0:T(8,128)} %bitcast.153), channel_id=1, source_target_pairs={{0,4},{4,0},{8,12},{12,8},{16,20},{20,16},{24,28},{28,24},{32,36},... | collective-permute-start | bytes 3145736 | tf_op jit(solution)/shard_map/ppermute | solution.py:77
  9.4 1.9 collective-permute-start.1
  11.4 0.8 concatenate.14
  12.3 0.4 collective-permute-done.1
  12.7 0.1 concatenate.15
  13.1 1.0 copy-done.3
  14.1 4.7 %shard_map.59 = f32[64,128,128]{2,1,0:T(8,128)} custom-call(f32[2,32,4096]{2,1,0:T(8,128)} %bitcast.154, f32[2,32,4096]{2,1,0:T(8,128)} %copy-done.3), custom_call_target="tpu_custom_call" | custom-call | tf_op jit(solution)/shard_map/pallas_call | solution.py:46
  18.9 4.4 %fusion.11 = f32[64,128,32]{1,2,0:T(8,128)} fusion(f32[64,128,128]{2,1,0:T(8,128)} %shard_map.59, f32[32,128,1]{1,0,2:T(8,128)S(1)} %reshape.132), kind=kOutput, calls=%fused_computation.69 | convolution fusion | flops 201326592 | bytes 5259264 | tf_op jit(solution)/shard_map/vq,jqo->jvo/dot_general | solution.py:19
  23.3 11.7 %all-to-all-start = ((f32[128,16,128]{2,1,0:T(8,128)}), f32[128,16,128]{2,1,0:T(8,128)S(1)}, u32[]{:S(2)}, u32[]{:S(2)}) async-start(f32[128,16,128]{2,1,0:T(8,128)} %bitcast.6), calls=%async_computation | async-start | bytes 2097152 | tf_op jit(solution)/shard_map/all_to_all | solution.py:104
  35.0 2.8 %collective-permute-start.2 = (f32[2,128,1024]{2,1,0:T(8,128)S(1)}, f32[2,128,1024]{2,1,0:T(8,128)S(1)}, u32[]{:S(2)}, u32[]{:S(2)}) collective-permute-start(f32[2,128,1024]{2,1,0:T(8,128)S(1)} %bitcast.156), channel_id=1, source_target_pairs={{0,4},{4,0},{8,12},{12,8},{16,20},{20,16},{24,28},{28,24},{32,36},... | collective-permute-start | bytes 3145736 | tf_op jit(solution)/shard_map/ppermute | solution.py:77
  37.8 0.2 dynamic-slice_reduce_fusion
  38.2 0.1 cosine_multiply_fusion
  38.3 1.8 collective-permute-done.2.other_ref
  40.1 1.0 copy-done.4
  41.0 4.7 %shard_map.60 = f32[16,512,128]{2,1,0:T(8,128)} custom-call(f32[2,128,1024]{2,1,0:T(8,128)} %bitcast.155, f32[2,128,1024]{2,1,0:T(8,128)} %copy-done.4), custom_call_target="tpu_custom_call" | custom-call | tf_op jit(solution)/shard_map/pallas_call | solution.py:46
  45.7 20.2 %all-to-all-done = f32[128,16,128]{2,1,0:T(8,128)S(1)} async-done(((f32[128,16,128]{2,1,0:T(8,128)}), f32[128,16,128]{2,1,0:T(8,128)S(1)}, u32[]{:S(2)}, u32[]{:S(2)}) %all-to-all-start) | async-done | bytes 1048608 | tf_op jit(solution)/shard_map/all_to_all | solution.py:104
  65.9 0.1 reduce_sum.70
  66.0 4.1 %convolution_bitcast_fusion.1 = f32[32,2,256]{2,0,1:T(8,128)S(1)} fusion(f32[2,256,128,16]{2,1,0,3:T(8,128)} %bitcast.145, f32[16,32,128]{2,1,0:T(8,128)S(1)} %bitcast_multiply_fusion.1), kind=kOutput, calls=%fused_computation.2 | convolution fusion | flops 201326592 | bytes 4521984 | tf_op jit(solution)/shard_map/ivo,iqo->ivq/dot_general | solution.py:19
  70.1 0.7 broadcast_in_dim.12
  70.8 4.0 %all-to-all-start.1 = ((f32[4,32,2,256]{3,1,2,0:T(8,128)}), f32[4,32,2,256]{3,1,2,0:T(8,128)S(1)}, u32[]{:S(2)}, u32[]{:S(2)}) async-start(f32[4,32,2,256]{3,1,2,0:T(8,128)} %broadcast_in_dim.12), calls=%async_computation.1 | async-start | bytes 524288 | tf_op jit(solution)/shard_map/all_to_all | solution.py:112
  74.9 5.9 %all-to-all-done.1 = f32[4,32,2,256]{3,1,2,0:T(8,128)S(1)} async-done(((f32[4,32,2,256]{3,1,2,0:T(8,128)}), f32[4,32,2,256]{3,1,2,0:T(8,128)S(1)}, u32[]{:S(2)}, u32[]{:S(2)}) %all-to-all-start.1) | async-done | bytes 262176 | tf_op jit(solution)/shard_map/all_to_all | solution.py:112
  80.8 1.1 multiply_reduce_fusion.3
  81.9 0.7 broadcast_in_dim.13
  82.6 18.8 %all_to_all.37 = f32[128,1,1]{2,1,0:T(1,128)S(1)} all-to-all(f32[128,1,1]{2,1,0:T(1,128)S(1)} %broadcast_in_dim.13), channel_id=1, replica_groups=mesh['tile'=128,'freq'=4] {'tile'}, dimensions={0} | all-to-all | bytes 1024 | tf_op jit(solution)/shard_map/all_to_all | solution.py:126
  101.4 0.7 reduce_sum.72
  102.9 0.5 multiply_reduce_fusion.1
  103.4 0.5 multiply_reduce_fusion.2
  104.0 3.5 %convolution_multiply_fusion = f32[16,128,32]{1,2,0:T(8,128)S(1)} fusion(f32[16,512,128]{2,1,0:T(8,128)} %shard_map.60, f32[32,512,1]{1,0,2:T(8,128)S(1)} %reshape.135, f32[16,128]{1,0:T(8,128)S(1)} %add_convert_fusion), kind=kOutput, calls=%fused_computation | convolution fusion | flops 201392128 | bytes 4530176 | tf_op jit(solution)/shard_map/vq,iqo->ivo/dot_general | solution.py:19
  107.6 0.1 broadcast_in_dim.15
  107.7 36.3 %all_to_all.38 = f32[128,16,128]{2,1,0:T(8,128)S(1)} all-to-all(f32[128,16,128]{2,1,0:T(8,128)S(1)} %bitcast.148), channel_id=1, replica_groups=mesh['tile'=128,'freq'=4] {'tile'}, dimensions={0} | all-to-all | bytes 2097152 | tf_op jit(solution)/shard_map/all_to_all | solution.py:144
  144.0 2.9 %fusion = f32[32,2,64]{2,0,1:T(8,128)S(1)} fusion(f32[32,2,64]{2,0,1:T(8,128)S(1)} %fusion.4, f32[64,32,128,1]{2,1,3,0:T(8,128)S(1)} %bitcast.151, f32[2,64,128,64]{2,1,0,3:T(8,128)S(1)} %bitcast.144), kind=kOutput, calls=%fused_computation.4 | convolution fusion | flops 201330688 | bytes 5275648 | tf_op jit(solution)/shard_map/jvo,jqo->jvq/dot_general | solution.py:19
  147.1 3.2 %fusion.12 = f32[64,128,32]{1,2,0:T(8,128)S(1)} fusion(f32[64,128,128]{2,1,0:T(8,128)} %shard_map.59, f32[32,128,1]{1,0,2:T(8,128)S(1)} %reshape.138), kind=kOutput, calls=%fused_computation.70 | convolution fusion | flops 201326592 | bytes 5259264 | tf_op jit(solution)/shard_map/vq,jqo->jvo/dot_general | solution.py:19
  150.3 37.2 %all_to_all.39 = f32[128,16,128]{2,1,0:T(8,128)S(1)} all-to-all(f32[128,16,128]{2,1,0:T(8,128)S(1)} %bitcast.147), channel_id=1, replica_groups=mesh['tile'=128,'freq'=4] {'tile'}, dimensions={0} | all-to-all | bytes 2097152 | tf_op jit(solution)/shard_map/all_to_all | solution.py:104
  187.5 0.1 reduce_sum.89
  187.7 4.1 %convolution_bitcast_fusion = f32[32,2,256]{2,0,1:T(8,128)S(1)} fusion(f32[2,256,128,16]{2,1,0,3:T(8,128)} %bitcast.146, f32[16,32,128]{2,1,0:T(8,128)S(1)} %bitcast_multiply_fusion), kind=kOutput, calls=%fused_computation.1 | convolution fusion | flops 201326592 | bytes 4521984 | tf_op jit(solution)/shard_map/ivo,iqo->ivq/dot_general | solution.py:19
  191.8 0.7 broadcast_in_dim.16
  192.5 3.4 %all-to-all-start.5 = ((f32[4,32,2,256]{3,1,2,0:T(8,128)}), f32[4,32,2,256]{3,1,2,0:T(8,128)S(1)}, u32[]{:S(2)}, u32[]{:S(2)}) async-start(f32[4,32,2,256]{3,1,2,0:T(8,128)} %broadcast_in_dim.16), calls=%async_computation.5 | async-start | bytes 524288 | tf_op jit(solution)/shard_map/all_to_all | solution.py:112
  196.0 2.2 collective-permute-start.4
  198.2 3.9 %all-to-all-done.5 = f32[4,32,2,256]{3,1,2,0:T(8,128)S(1)} async-done(((f32[4,32,2,256]{3,1,2,0:T(8,128)}), f32[4,32,2,256]{3,1,2,0:T(8,128)S(1)}, u32[]{:S(2)}, u32[]{:S(2)}) %all-to-all-start.5) | async-done | bytes 262176 | tf_op jit(solution)/shard_map/all_to_all | solution.py:112
  202.1 1.5 multiply_reduce_fusion
  203.6 1.3 broadcast_in_dim.17
  204.9 7.3 %all-to-all-start.6 = ((f32[128,1,1]{2,1,0:T(1,128)}), f32[128,1,1]{2,1,0:T(1,128)S(1)}, u32[]{:S(2)}, u32[]{:S(2)}) async-start(f32[128,1,1]{2,1,0:T(1,128)} %broadcast_in_dim.17), calls=%async_computation.6 | async-start | bytes 131072 | tf_op jit(solution)/shard_map/all_to_all | solution.py:126
  212.2 11.4 %all-to-all-done.6 = f32[128,1,1]{2,1,0:T(1,128)S(1)} async-done(((f32[128,1,1]{2,1,0:T(1,128)}), f32[128,1,1]{2,1,0:T(1,128)S(1)}, u32[]{:S(2)}, u32[]{:S(2)}) %all-to-all-start.6) | async-done | bytes 544 | tf_op jit(solution)/shard_map/all_to_all | solution.py:126
  223.6 0.7 reduce_sum.91
  225.1 0.1 fusion.10
  225.3 2.5 %collective-permute-start.3 = (f32[4,2,16,128]{3,2,1,0:T(8,128)S(1)}, f32[4,2,16,128]{3,2,1,0:T(8,128)S(1)}, u32[]{:S(2)}, u32[]{:S(2)}) collective-permute-start(f32[4,2,16,128]{3,2,1,0:T(8,128)S(1)} %bitcast.159), channel_id=1, source_target_pairs={{0,4},{4,0},{8,12},{12,8},{16,20},{20,16},{24,28},{28,24},{32,36},... | collective-permute-start | bytes 196616 | tf_op jit(solution)/shard_map/ppermute | solution.py:77
  227.9 0.7 reshape.131
  228.7 0.8 copy.49
  (40 shorter events, 1.3 us)
Async XLA Ops:
  0.6 37.2 %copy-start = (s32[1,16,64]{2,1,0:T(8,128)S(1)}, s32[1,16,64]{2,1,0:T(8,128)}, u32[]{:S(2)}) copy-start(s32[1,16,64]{2,1,0:T(8,128)} %param.7) | copy-start | bytes 12292
  0.6 12.5 %collective-permute-start = (f32[2,32,4096]{2,1,0:T(8,128)}, f32[2,32,4096]{2,1,0:T(8,128)S(1)}, u32[]{:S(2)}, u32[]{:S(2)}) collective-permute-start(f32[2,32,4096]{2,1,0:T(8,128)} %bitcast.153), channel_id=1, source_target_pairs={{0,4},{4,0},{8,12},{12,8},{16,20},{20,16},{24,28},{28,24},{32,36},... | collective-permute-start | bytes 3145736 | tf_op jit(solution)/shard_map/ppermute | solution.py:77
  9.4 3.3 %collective-permute-start.1 = (f32[32,128]{1,0:T(8,128)}, f32[32,128]{1,0:T(8,128)S(1)}, u32[]{:S(2)}, u32[]{:S(2)}) collective-permute-start(f32[32,128]{1,0:T(8,128)} %bitcast.160), channel_id=1, source_target_pairs={{0,4},{4,0},{8,12},{12,8},{16,20},{20,16},{24,28},{28,24},{32,36},... | collective-permute-start | bytes 49160 | tf_op jit(solution)/shard_map/ppermute | solution.py:77
  13.1 1.0 copy-start.3
  18.9 16.1 %copy-start.2 = (f32[2,1,128,1024]{3,2,1,0:T(8,128)S(1)}, f32[2,1,128,1024]{3,2,1,0:T(8,128)}, u32[]{:S(2)}) copy-start(f32[2,1,128,1024]{3,2,1,0:T(8,128)} %param.6) | copy-start | bytes 3145732
  23.3 42.6 %all-to-all-start = ((f32[128,16,128]{2,1,0:T(8,128)}), f32[128,16,128]{2,1,0:T(8,128)S(1)}, u32[]{:S(2)}, u32[]{:S(2)}) async-start(f32[128,16,128]{2,1,0:T(8,128)} %bitcast.6), calls=%async_computation | async-start | bytes 2097152 | tf_op jit(solution)/shard_map/all_to_all | solution.py:104
  35.0 5.1 %collective-permute-start.2 = (f32[2,128,1024]{2,1,0:T(8,128)S(1)}, f32[2,128,1024]{2,1,0:T(8,128)S(1)}, u32[]{:S(2)}, u32[]{:S(2)}) collective-permute-start(f32[2,128,1024]{2,1,0:T(8,128)S(1)} %bitcast.156), channel_id=1, source_target_pairs={{0,4},{4,0},{8,12},{12,8},{16,20},{20,16},{24,28},{28,24},{32,36},... | collective-permute-start | bytes 3145736 | tf_op jit(solution)/shard_map/ppermute | solution.py:77
  40.1 1.0 copy-start.4
  70.8 9.9 %all-to-all-start.1 = ((f32[4,32,2,256]{3,1,2,0:T(8,128)}), f32[4,32,2,256]{3,1,2,0:T(8,128)S(1)}, u32[]{:S(2)}, u32[]{:S(2)}) async-start(f32[4,32,2,256]{3,1,2,0:T(8,128)} %broadcast_in_dim.12), calls=%async_computation.1 | async-start | bytes 524288 | tf_op jit(solution)/shard_map/all_to_all | solution.py:112
  104.0 40.0 %copy-start.1 = (f32[64,128,128]{2,1,0:T(8,128)S(1)}, f32[64,128,128]{2,1,0:T(8,128)}, u32[]{:S(2)}) copy-start(f32[64,128,128]{2,1,0:T(8,128)} %shard_map.59) | copy-start | bytes 12582916
  192.5 9.6 %all-to-all-start.5 = ((f32[4,32,2,256]{3,1,2,0:T(8,128)}), f32[4,32,2,256]{3,1,2,0:T(8,128)S(1)}, u32[]{:S(2)}, u32[]{:S(2)}) async-start(f32[4,32,2,256]{3,1,2,0:T(8,128)} %broadcast_in_dim.16), calls=%async_computation.5 | async-start | bytes 524288 | tf_op jit(solution)/shard_map/all_to_all | solution.py:112
  196.0 16.2 %collective-permute-start.4 = (f32[32,2,32]{2,0,1:T(8,128)S(1)}, f32[32,2,32]{2,0,1:T(8,128)S(1)}, u32[]{:S(2)}, u32[]{:S(2)}) collective-permute-start(f32[32,2,32]{2,0,1:T(8,128)S(1)} %slice.155), channel_id=1, source_target_pairs={{0,4},{4,0},{8,12},{12,8},{16,20},{20,16},{24,28},{28,24},{32,36},... | collective-permute-start | bytes 24584 | tf_op jit(solution)/shard_map/ppermute | solution.py:77
  204.9 18.7 %all-to-all-start.6 = ((f32[128,1,1]{2,1,0:T(1,128)}), f32[128,1,1]{2,1,0:T(1,128)S(1)}, u32[]{:S(2)}, u32[]{:S(2)}) async-start(f32[128,1,1]{2,1,0:T(1,128)} %broadcast_in_dim.17), calls=%async_computation.6 | async-start | bytes 131072 | tf_op jit(solution)/shard_map/all_to_all | solution.py:126
  225.3 3.4 %collective-permute-start.3 = (f32[4,2,16,128]{3,2,1,0:T(8,128)S(1)}, f32[4,2,16,128]{3,2,1,0:T(8,128)S(1)}, u32[]{:S(2)}, u32[]{:S(2)}) collective-permute-start(f32[4,2,16,128]{3,2,1,0:T(8,128)S(1)} %bitcast.159), channel_id=1, source_target_pairs={{0,4},{4,0},{8,12},{12,8},{16,20},{20,16},{24,28},{28,24},{32,36},... | collective-permute-start | bytes 196616 | tf_op jit(solution)/shard_map/ppermute | solution.py:77

commit v4 on v3

--- a/solution.py
+++ b/solution.py
@@ -41,7 +41,7 @@
 def build_weights(own, other):
     rows, cols = own.shape[1], own.shape[2]
     tiles = cols // R
-    per_step = min(tiles, 16)
+    per_step = min(tiles, 32)
     spec = pl.BlockSpec((2, rows, per_step * R), lambda p: (0, 0, p))
     return pl.pallas_call(
         weight_kernel,

time: 230 us -> 229 us (level)
  no operation moved by 1% of the time
where the time goes in v4:
time: 229 us; the launch traced here: 228 us
  blocking collectives  92.2 us (40%)
  starting transfers between devices  44.8 us (20%)
  waiting for transfers between devices  43.4 us (19%)
  matrix products  22.3 us (10%)
  local copies, waits for them, and re-layouts  9.01 us (4%)
  Pallas kernels  8.4 us (4%)
  other arithmetic  5.78 us (3%)
  between operations  2.45 us (1%)
    all_to_all x1, blocking collectives, adjoint(): incoming = lax.all_to_all(outgoing, 'tile', 0, 0, tiled=True)  37.2 us
    all_to_all x1, blocking collectives, local(): incoming = lax.all_to_all(outgoing, 'tile', 0, 0, tiled=True)  36.1 us
    dot_general x6, matrix products, contract(): return jnp.einsum(form, left, right, precision=matmul_precision)  22.3 us
    all_to_all x1, waiting for transfers between devices, adjoint(): incoming = lax.all_to_all(outgoing, 'tile', 0, 0, tiled=True)  20.2 us
    all_to_all x1, blocking collectives, threshold_of(): total = jnp.sum(lax.all_to_all(outgoing, 'tile', 0, 0, tiled=True))  18.9 us
    ppermute x5, starting transfers between devices, swap(): return lax.ppermute(x, 'tile', pair)  18.4 us
    all_to_all x1, starting transfers between devices, adjoint(): incoming = lax.all_to_all(outgoing, 'tile', 0, 0, tiled=True)  11.7 us
    all_to_all x1, waiting for transfers between devices, threshold_of(): total = jnp.sum(lax.all_to_all(outgoing, 'tile', 0, 0, tiled=True))  11.4 us
  transfers between devices with their start and end apart: 9, of which 6 were waited for; matrix products, arithmetic and copies ran while one was open for 2% of the time, Pallas kernels for 2%

profile of v4, /device:TPU:1, one launch (start us, length us, event | category | flops | bytes accessed | tf_op | source)
XLA Modules:
  0.0 228.2 jit_solution(10641309469760093350)
XLA Ops:
  0.6 8.8 %collective-permute-start = (f32[2,32,4096]{2,1,0:T(8,128)}, f32[2,32,4096]{2,1,0:T(8,128)S(1)}, u32[]{:S(2)}, u32[]{:S(2)}) collective-permute-start(f32[2,32,4096]{2,1,0:T(8,128)} %bitcast.153), channel_id=1, source_target_pairs={{0,4},{4,0},{8,12},{12,8},{16,20},{20,16},{24,28},{28,24},{32,36},... | collective-permute-start | bytes 3145736 | tf_op jit(solution)/shard_map/ppermute | solution.py:77
  9.4 1.9 collective-permute-start.1
  11.4 0.8 concatenate.14
  12.3 0.4 collective-permute-done.1
  12.7 0.1 concatenate.15
  13.1 1.0 copy-done.3
  14.1 3.7 %shard_map.59 = f32[64,128,128]{2,1,0:T(8,128)} custom-call(f32[2,32,4096]{2,1,0:T(8,128)} %bitcast.154, f32[2,32,4096]{2,1,0:T(8,128)} %copy-done.3), custom_call_target="tpu_custom_call" | custom-call | tf_op jit(solution)/shard_map/pallas_call | solution.py:46
  17.9 4.4 %fusion.11 = f32[64,128,32]{1,2,0:T(8,128)} fusion(f32[64,128,128]{2,1,0:T(8,128)} %shard_map.59, f32[32,128,1]{1,0,2:T(8,128)S(1)} %reshape.132), kind=kOutput, calls=%fused_computation.69 | convolution fusion | flops 201326592 | bytes 5259264 | tf_op jit(solution)/shard_map/vq,jqo->jvo/dot_general | solution.py:19
  22.2 11.7 %all-to-all-start = ((f32[128,16,128]{2,1,0:T(8,128)}), f32[128,16,128]{2,1,0:T(8,128)S(1)}, u32[]{:S(2)}, u32[]{:S(2)}) async-start(f32[128,16,128]{2,1,0:T(8,128)} %bitcast.6), calls=%async_computation | async-start | bytes 2097152 | tf_op jit(solution)/shard_map/all_to_all | solution.py:104
  34.0 2.8 %collective-permute-start.2 = (f32[2,128,1024]{2,1,0:T(8,128)S(1)}, f32[2,128,1024]{2,1,0:T(8,128)S(1)}, u32[]{:S(2)}, u32[]{:S(2)}) collective-permute-start(f32[2,128,1024]{2,1,0:T(8,128)S(1)} %bitcast.156), channel_id=1, source_target_pairs={{0,4},{4,0},{8,12},{12,8},{16,20},{20,16},{24,28},{28,24},{32,36},... | collective-permute-start | bytes 3145736 | tf_op jit(solution)/shard_map/ppermute | solution.py:77
  36.8 0.2 dynamic-slice_reduce_fusion
  37.2 0.1 cosine_multiply_fusion
  37.3 1.8 collective-permute-done.2.other_ref
  39.0 1.0 copy-done.4
  40.0 4.7 %shard_map.60 = f32[16,512,128]{2,1,0:T(8,128)} custom-call(f32[2,128,1024]{2,1,0:T(8,128)} %bitcast.155, f32[2,128,1024]{2,1,0:T(8,128)} %copy-done.4), custom_call_target="tpu_custom_call" | custom-call | tf_op jit(solution)/shard_map/pallas_call | solution.py:46
  44.7 20.2 %all-to-all-done = f32[128,16,128]{2,1,0:T(8,128)S(1)} async-done(((f32[128,16,128]{2,1,0:T(8,128)}), f32[128,16,128]{2,1,0:T(8,128)S(1)}, u32[]{:S(2)}, u32[]{:S(2)}) %all-to-all-start) | async-done | bytes 1048608 | tf_op jit(solution)/shard_map/all_to_all | solution.py:104
  64.9 0.1 reduce_sum.70
  65.0 4.1 %convolution_bitcast_fusion.1 = f32[32,2,256]{2,0,1:T(8,128)S(1)} fusion(f32[2,256,128,16]{2,1,0,3:T(8,128)} %bitcast.145, f32[16,32,128]{2,1,0:T(8,128)S(1)} %bitcast_multiply_fusion.1), kind=kOutput, calls=%fused_computation.2 | convolution fusion | flops 201326592 | bytes 4521984 | tf_op jit(solution)/shard_map/ivo,iqo->ivq/dot_general | solution.py:19
  69.1 0.7 broadcast_in_dim.12
  69.8 4.0 %all-to-all-start.1 = ((f32[4,32,2,256]{3,1,2,0:T(8,128)}), f32[4,32,2,256]{3,1,2,0:T(8,128)S(1)}, u32[]{:S(2)}, u32[]{:S(2)}) async-start(f32[4,32,2,256]{3,1,2,0:T(8,128)} %broadcast_in_dim.12), calls=%async_computation.1 | async-start | bytes 524288 | tf_op jit(solution)/shard_map/all_to_all | solution.py:112
  73.9 5.9 %all-to-all-done.1 = f32[4,32,2,256]{3,1,2,0:T(8,128)S(1)} async-done(((f32[4,32,2,256]{3,1,2,0:T(8,128)}), f32[4,32,2,256]{3,1,2,0:T(8,128)S(1)}, u32[]{:S(2)}, u32[]{:S(2)}) %all-to-all-start.1) | async-done | bytes 262176 | tf_op jit(solution)/shard_map/all_to_all | solution.py:112
  79.8 1.1 multiply_reduce_fusion.3
  80.9 0.7 broadcast_in_dim.13
  81.6 18.9 %all_to_all.37 = f32[128,1,1]{2,1,0:T(1,128)S(1)} all-to-all(f32[128,1,1]{2,1,0:T(1,128)S(1)} %broadcast_in_dim.13), channel_id=1, replica_groups=mesh['tile'=128,'freq'=4] {'tile'}, dimensions={0} | all-to-all | bytes 1024 | tf_op jit(solution)/shard_map/all_to_all | solution.py:126
  100.4 0.7 reduce_sum.72
  101.9 0.5 multiply_reduce_fusion.1
  102.4 0.5 multiply_reduce_fusion.2
  103.0 3.5 %convolution_multiply_fusion = f32[16,128,32]{1,2,0:T(8,128)S(1)} fusion(f32[16,512,128]{2,1,0:T(8,128)} %shard_map.60, f32[32,512,1]{1,0,2:T(8,128)S(1)} %reshape.135, f32[16,128]{1,0:T(8,128)S(1)} %add_convert_fusion), kind=kOutput, calls=%fused_computation | convolution fusion | flops 201392128 | bytes 4530176 | tf_op jit(solution)/shard_map/vq,iqo->ivo/dot_general | solution.py:19
  106.6 0.1 broadcast_in_dim.15
  106.7 36.1 %all_to_all.38 = f32[128,16,128]{2,1,0:T(8,128)S(1)} all-to-all(f32[128,16,128]{2,1,0:T(8,128)S(1)} %bitcast.148), channel_id=1, replica_groups=mesh['tile'=128,'freq'=4] {'tile'}, dimensions={0} | all-to-all | bytes 2097152 | tf_op jit(solution)/shard_map/all_to_all | solution.py:144
  142.8 2.9 %fusion = f32[32,2,64]{2,0,1:T(8,128)S(1)} fusion(f32[32,2,64]{2,0,1:T(8,128)S(1)} %fusion.4, f32[64,32,128,1]{2,1,3,0:T(8,128)S(1)} %bitcast.151, f32[2,64,128,64]{2,1,0,3:T(8,128)S(1)} %bitcast.144), kind=kOutput, calls=%fused_computation.4 | convolution fusion | flops 201330688 | bytes 5275648 | tf_op jit(solution)/shard_map/jvo,jqo->jvq/dot_general | solution.py:19
  145.9 3.2 %fusion.12 = f32[64,128,32]{1,2,0:T(8,128)S(1)} fusion(f32[64,128,128]{2,1,0:T(8,128)} %shard_map.59, f32[32,128,1]{1,0,2:T(8,128)S(1)} %reshape.138), kind=kOutput, calls=%fused_computation.70 | convolution fusion | flops 201326592 | bytes 5259264 | tf_op jit(solution)/shard_map/vq,jqo->jvo/dot_general | solution.py:19
  149.1 37.2 %all_to_all.39 = f32[128,16,128]{2,1,0:T(8,128)S(1)} all-to-all(f32[128,16,128]{2,1,0:T(8,128)S(1)} %bitcast.147), channel_id=1, replica_groups=mesh['tile'=128,'freq'=4] {'tile'}, dimensions={0} | all-to-all | bytes 2097152 | tf_op jit(solution)/shard_map/all_to_all | solution.py:104
  186.3 0.1 reduce_sum.89
  186.5 4.1 %convolution_bitcast_fusion = f32[32,2,256]{2,0,1:T(8,128)S(1)} fusion(f32[2,256,128,16]{2,1,0,3:T(8,128)} %bitcast.146, f32[16,32,128]{2,1,0:T(8,128)S(1)} %bitcast_multiply_fusion), kind=kOutput, calls=%fused_computation.1 | convolution fusion | flops 201326592 | bytes 4521984 | tf_op jit(solution)/shard_map/ivo,iqo->ivq/dot_general | solution.py:19
  190.6 0.7 broadcast_in_dim.16
  191.3 3.4 %all-to-all-start.5 = ((f32[4,32,2,256]{3,1,2,0:T(8,128)}), f32[4,32,2,256]{3,1,2,0:T(8,128)S(1)}, u32[]{:S(2)}, u32[]{:S(2)}) async-start(f32[4,32,2,256]{3,1,2,0:T(8,128)} %broadcast_in_dim.16), calls=%async_computation.5 | async-start | bytes 524288 | tf_op jit(solution)/shard_map/all_to_all | solution.py:112
  194.8 2.4 %collective-permute-start.4 = (f32[32,2,32]{2,0,1:T(8,128)S(1)}, f32[32,2,32]{2,0,1:T(8,128)S(1)}, u32[]{:S(2)}, u32[]{:S(2)}) collective-permute-start(f32[32,2,32]{2,0,1:T(8,128)S(1)} %slice.155), channel_id=1, source_target_pairs={{0,4},{4,0},{8,12},{12,8},{16,20},{20,16},{24,28},{28,24},{32,36},... | collective-permute-start | bytes 24584 | tf_op jit(solution)/shard_map/ppermute | solution.py:77
  197.2 3.7 %all-to-all-done.5 = f32[4,32,2,256]{3,1,2,0:T(8,128)S(1)} async-done(((f32[4,32,2,256]{3,1,2,0:T(8,128)}), f32[4,32,2,256]{3,1,2,0:T(8,128)S(1)}, u32[]{:S(2)}, u32[]{:S(2)}) %all-to-all-start.5) | async-done | bytes 262176 | tf_op jit(solution)/shard_map/all_to_all | solution.py:112
  200.9 1.5 multiply_reduce_fusion
  202.4 1.3 broadcast_in_dim.17
  203.7 7.3 %all-to-all-start.6 = ((f32[128,1,1]{2,1,0:T(1,128)}), f32[128,1,1]{2,1,0:T(1,128)S(1)}, u32[]{:S(2)}, u32[]{:S(2)}) async-start(f32[128,1,1]{2,1,0:T(1,128)} %broadcast_in_dim.17), calls=%async_computation.6 | async-start | bytes 131072 | tf_op jit(solution)/shard_map/all_to_all | solution.py:126
  211.1 11.4 %all-to-all-done.6 = f32[128,1,1]{2,1,0:T(1,128)S(1)} async-done(((f32[128,1,1]{2,1,0:T(1,128)}), f32[128,1,1]{2,1,0:T(1,128)S(1)}, u32[]{:S(2)}, u32[]{:S(2)}) %all-to-all-start.6) | async-done | bytes 544 | tf_op jit(solution)/shard_map/all_to_all | solution.py:126
  222.4 0.7 reduce_sum.91
  223.9 0.1 fusion.10
  224.1 2.5 %collective-permute-start.3 = (f32[4,2,16,128]{3,2,1,0:T(8,128)S(1)}, f32[4,2,16,128]{3,2,1,0:T(8,128)S(1)}, u32[]{:S(2)}, u32[]{:S(2)}) collective-permute-start(f32[4,2,16,128]{3,2,1,0:T(8,128)S(1)} %bitcast.159), channel_id=1, source_target_pairs={{0,4},{4,0},{8,12},{12,8},{16,20},{20,16},{24,28},{28,24},{32,36},... | collective-permute-start | bytes 196616 | tf_op jit(solution)/shard_map/ppermute | solution.py:77
  226.7 0.7 reshape.131
  227.5 0.8 copy.49
  (40 shorter events, 1.3 us)
Async XLA Ops:
  0.6 36.2 %copy-start = (s32[1,16,64]{2,1,0:T(8,128)S(1)}, s32[1,16,64]{2,1,0:T(8,128)}, u32[]{:S(2)}) copy-start(s32[1,16,64]{2,1,0:T(8,128)} %param.7) | copy-start | bytes 12292
  0.6 12.5 %collective-permute-start = (f32[2,32,4096]{2,1,0:T(8,128)}, f32[2,32,4096]{2,1,0:T(8,128)S(1)}, u32[]{:S(2)}, u32[]{:S(2)}) collective-permute-start(f32[2,32,4096]{2,1,0:T(8,128)} %bitcast.153), channel_id=1, source_target_pairs={{0,4},{4,0},{8,12},{12,8},{16,20},{20,16},{24,28},{28,24},{32,36},... | collective-permute-start | bytes 3145736 | tf_op jit(solution)/shard_map/ppermute | solution.py:77
  9.4 3.3 %collective-permute-start.1 = (f32[32,128]{1,0:T(8,128)}, f32[32,128]{1,0:T(8,128)S(1)}, u32[]{:S(2)}, u32[]{:S(2)}) collective-permute-start(f32[32,128]{1,0:T(8,128)} %bitcast.160), channel_id=1, source_target_pairs={{0,4},{4,0},{8,12},{12,8},{16,20},{20,16},{24,28},{28,24},{32,36},... | collective-permute-start | bytes 49160 | tf_op jit(solution)/shard_map/ppermute | solution.py:77
  13.1 1.0 copy-start.3
  17.9 16.1 %copy-start.2 = (f32[2,1,128,1024]{3,2,1,0:T(8,128)S(1)}, f32[2,1,128,1024]{3,2,1,0:T(8,128)}, u32[]{:S(2)}) copy-start(f32[2,1,128,1024]{3,2,1,0:T(8,128)} %param.6) | copy-start | bytes 3145732
  22.2 42.6 %all-to-all-start = ((f32[128,16,128]{2,1,0:T(8,128)}), f32[128,16,128]{2,1,0:T(8,128)S(1)}, u32[]{:S(2)}, u32[]{:S(2)}) async-start(f32[128,16,128]{2,1,0:T(8,128)} %bitcast.6), calls=%async_computation | async-start | bytes 2097152 | tf_op jit(solution)/shard_map/all_to_all | solution.py:104
  34.0 5.1 %collective-permute-start.2 = (f32[2,128,1024]{2,1,0:T(8,128)S(1)}, f32[2,128,1024]{2,1,0:T(8,128)S(1)}, u32[]{:S(2)}, u32[]{:S(2)}) collective-permute-start(f32[2,128,1024]{2,1,0:T(8,128)S(1)} %bitcast.156), channel_id=1, source_target_pairs={{0,4},{4,0},{8,12},{12,8},{16,20},{20,16},{24,28},{28,24},{32,36},... | collective-permute-start | bytes 3145736 | tf_op jit(solution)/shard_map/ppermute | solution.py:77
  39.0 1.0 copy-start.4
  69.8 9.9 %all-to-all-start.1 = ((f32[4,32,2,256]{3,1,2,0:T(8,128)}), f32[4,32,2,256]{3,1,2,0:T(8,128)S(1)}, u32[]{:S(2)}, u32[]{:S(2)}) async-start(f32[4,32,2,256]{3,1,2,0:T(8,128)} %broadcast_in_dim.12), calls=%async_computation.1 | async-start | bytes 524288 | tf_op jit(solution)/shard_map/all_to_all | solution.py:112
  103.0 39.8 %copy-start.1 = (f32[64,128,128]{2,1,0:T(8,128)S(1)}, f32[64,128,128]{2,1,0:T(8,128)}, u32[]{:S(2)}) copy-start(f32[64,128,128]{2,1,0:T(8,128)} %shard_map.59) | copy-start | bytes 12582916
  191.3 9.6 %all-to-all-start.5 = ((f32[4,32,2,256]{3,1,2,0:T(8,128)}), f32[4,32,2,256]{3,1,2,0:T(8,128)S(1)}, u32[]{:S(2)}, u32[]{:S(2)}) async-start(f32[4,32,2,256]{3,1,2,0:T(8,128)} %broadcast_in_dim.16), calls=%async_computation.5 | async-start | bytes 524288 | tf_op jit(solution)/shard_map/all_to_all | solution.py:112
  194.8 16.2 %collective-permute-start.4 = (f32[32,2,32]{2,0,1:T(8,128)S(1)}, f32[32,2,32]{2,0,1:T(8,128)S(1)}, u32[]{:S(2)}, u32[]{:S(2)}) collective-permute-start(f32[32,2,32]{2,0,1:T(8,128)S(1)} %slice.155), channel_id=1, source_target_pairs={{0,4},{4,0},{8,12},{12,8},{16,20},{20,16},{24,28},{28,24},{32,36},... | collective-permute-start | bytes 24584 | tf_op jit(solution)/shard_map/ppermute | solution.py:77
  203.7 18.7 %all-to-all-start.6 = ((f32[128,1,1]{2,1,0:T(1,128)}), f32[128,1,1]{2,1,0:T(1,128)S(1)}, u32[]{:S(2)}, u32[]{:S(2)}) async-start(f32[128,1,1]{2,1,0:T(1,128)} %broadcast_in_dim.17), calls=%async_computation.6 | async-start | bytes 131072 | tf_op jit(solution)/shard_map/all_to_all | solution.py:126
  224.1 3.4 %collective-permute-start.3 = (f32[4,2,16,128]{3,2,1,0:T(8,128)S(1)}, f32[4,2,16,128]{3,2,1,0:T(8,128)S(1)}, u32[]{:S(2)}, u32[]{:S(2)}) collective-permute-start(f32[4,2,16,128]{3,2,1,0:T(8,128)S(1)} %bitcast.159), channel_id=1, source_target_pairs={{0,4},{4,0},{8,12},{12,8},{16,20},{20,16},{24,28},{28,24},{32,36},... | collective-permute-start | bytes 196616 | tf_op jit(solution)/shard_map/ppermute | solution.py:77

commit v5 on v4

--- a/solution.py
+++ b/solution.py
@@ -41,7 +41,7 @@
 def build_weights(own, other):
     rows, cols = own.shape[1], own.shape[2]
     tiles = cols // R
-    per_step = min(tiles, 32)
+    per_step = tiles
     spec = pl.BlockSpec((2, rows, per_step * R), lambda p: (0, 0, p))
     return pl.pallas_call(
         weight_kernel,

time: 229 us -> 230 us (level)
  no operation moved by 1% of the time
where the time goes in v5:
time: 230 us; the launch traced here: 229 us
  blocking collectives  92.2 us (40%)
  starting transfers between devices  44.8 us (19%)
  waiting for transfers between devices  43.4 us (19%)
  matrix products  22.3 us (10%)
  Pallas kernels  9.27 us (4%)
  local copies, waits for them, and re-layouts  9.01 us (4%)
  other arithmetic  5.78 us (3%)
  between operations  2.45 us (1%)
    all_to_all x1, blocking collectives, adjoint(): incoming = lax.all_to_all(outgoing, 'tile', 0, 0, tiled=True)  37.2 us
    all_to_all x1, blocking collectives, local(): incoming = lax.all_to_all(outgoing, 'tile', 0, 0, tiled=True)  36.1 us
    dot_general x6, matrix products, contract(): return jnp.einsum(form, left, right, precision=matmul_precision)  22.3 us
    all_to_all x1, waiting for transfers between devices, adjoint(): incoming = lax.all_to_all(outgoing, 'tile', 0, 0, tiled=True)  20.2 us
    all_to_all x1, blocking collectives, threshold_of(): total = jnp.sum(lax.all_to_all(outgoing, 'tile', 0, 0, tiled=True))  18.9 us
    ppermute x5, starting transfers between devices, swap(): return lax.ppermute(x, 'tile', pair)  18.4 us
    all_to_all x1, starting transfers between devices, adjoint(): incoming = lax.all_to_all(outgoing, 'tile', 0, 0, tiled=True)  11.7 us
    all_to_all x1, waiting for transfers between devices, threshold_of(): total = jnp.sum(lax.all_to_all(outgoing, 'tile', 0, 0, tiled=True))  11.4 us
  transfers between devices with their start and end apart: 9, of which 6 were waited for; matrix products, arithmetic and copies ran while one was open for 2% of the time, Pallas kernels for 2%

profile of v5, /device:TPU:1, one launch (start us, length us, event | category | flops | bytes accessed | tf_op | source)
XLA Modules:
  0.0 229.1 jit_solution(8015171206438251116)
XLA Ops:
  0.6 8.8 %collective-permute-start = (f32[2,32,4096]{2,1,0:T(8,128)}, f32[2,32,4096]{2,1,0:T(8,128)S(1)}, u32[]{:S(2)}, u32[]{:S(2)}) collective-permute-start(f32[2,32,4096]{2,1,0:T(8,128)} %bitcast.153), channel_id=1, source_target_pairs={{0,4},{4,0},{8,12},{12,8},{16,20},{20,16},{24,28},{28,24},{32,36},... | collective-permute-start | bytes 3145736 | tf_op jit(solution)/shard_map/ppermute | solution.py:77
  9.4 1.9 collective-permute-start.1
  11.4 0.8 concatenate.14
  12.3 0.4 collective-permute-done.1
  12.7 0.1 concatenate.15
  13.1 1.0 copy-done.3
  14.1 4.6 %shard_map.59 = f32[64,128,128]{2,1,0:T(8,128)} custom-call(f32[2,32,4096]{2,1,0:T(8,128)} %bitcast.154, f32[2,32,4096]{2,1,0:T(8,128)} %copy-done.3), custom_call_target="tpu_custom_call" | custom-call | tf_op jit(solution)/shard_map/pallas_call | solution.py:46
  18.7 4.4 %fusion.11 = f32[64,128,32]{1,2,0:T(8,128)} fusion(f32[64,128,128]{2,1,0:T(8,128)} %shard_map.59, f32[32,128,1]{1,0,2:T(8,128)S(1)} %reshape.132), kind=kOutput, calls=%fused_computation.69 | convolution fusion | flops 201326592 | bytes 5259264 | tf_op jit(solution)/shard_map/vq,jqo->jvo/dot_general | solution.py:19
  23.1 11.7 %all-to-all-start = ((f32[128,16,128]{2,1,0:T(8,128)}), f32[128,16,128]{2,1,0:T(8,128)S(1)}, u32[]{:S(2)}, u32[]{:S(2)}) async-start(f32[128,16,128]{2,1,0:T(8,128)} %bitcast.6), calls=%async_computation | async-start | bytes 2097152 | tf_op jit(solution)/shard_map/all_to_all | solution.py:104
  34.8 2.8 %collective-permute-start.2 = (f32[2,128,1024]{2,1,0:T(8,128)S(1)}, f32[2,128,1024]{2,1,0:T(8,128)S(1)}, u32[]{:S(2)}, u32[]{:S(2)}) collective-permute-start(f32[2,128,1024]{2,1,0:T(8,128)S(1)} %bitcast.156), channel_id=1, source_target_pairs={{0,4},{4,0},{8,12},{12,8},{16,20},{20,16},{24,28},{28,24},{32,36},... | collective-permute-start | bytes 3145736 | tf_op jit(solution)/shard_map/ppermute | solution.py:77
  37.7 0.2 dynamic-slice_reduce_fusion
  38.0 0.1 cosine_multiply_fusion
  38.2 1.8 collective-permute-done.2.other_ref
  39.9 1.0 copy-done.4
  40.9 4.7 %shard_map.60 = f32[16,512,128]{2,1,0:T(8,128)} custom-call(f32[2,128,1024]{2,1,0:T(8,128)} %bitcast.155, f32[2,128,1024]{2,1,0:T(8,128)} %copy-done.4), custom_call_target="tpu_custom_call" | custom-call | tf_op jit(solution)/shard_map/pallas_call | solution.py:46
  45.6 20.2 %all-to-all-done = f32[128,16,128]{2,1,0:T(8,128)S(1)} async-done(((f32[128,16,128]{2,1,0:T(8,128)}), f32[128,16,128]{2,1,0:T(8,128)S(1)}, u32[]{:S(2)}, u32[]{:S(2)}) %all-to-all-start) | async-done | bytes 1048608 | tf_op jit(solution)/shard_map/all_to_all | solution.py:104
  65.7 0.1 reduce_sum.70
  65.9 4.1 %convolution_bitcast_fusion.1 = f32[32,2,256]{2,0,1:T(8,128)S(1)} fusion(f32[2,256,128,16]{2,1,0,3:T(8,128)} %bitcast.145, f32[16,32,128]{2,1,0:T(8,128)S(1)} %bitcast_multiply_fusion.1), kind=kOutput, calls=%fused_computation.2 | convolution fusion | flops 201326592 | bytes 4521984 | tf_op jit(solution)/shard_map/ivo,iqo->ivq/dot_general | solution.py:19
  70.0 0.7 broadcast_in_dim.12
  70.7 4.0 %all-to-all-start.1 = ((f32[4,32,2,256]{3,1,2,0:T(8,128)}), f32[4,32,2,256]{3,1,2,0:T(8,128)S(1)}, u32[]{:S(2)}, u32[]{:S(2)}) async-start(f32[4,32,2,256]{3,1,2,0:T(8,128)} %broadcast_in_dim.12), calls=%async_computation.1 | async-start | bytes 524288 | tf_op jit(solution)/shard_map/all_to_all | solution.py:112
  74.7 5.9 %all-to-all-done.1 = f32[4,32,2,256]{3,1,2,0:T(8,128)S(1)} async-done(((f32[4,32,2,256]{3,1,2,0:T(8,128)}), f32[4,32,2,256]{3,1,2,0:T(8,128)S(1)}, u32[]{:S(2)}, u32[]{:S(2)}) %all-to-all-start.1) | async-done | bytes 262176 | tf_op jit(solution)/shard_map/all_to_all | solution.py:112
  80.7 1.1 multiply_reduce_fusion.3
  81.8 0.7 broadcast_in_dim.13
  82.4 18.9 %all_to_all.37 = f32[128,1,1]{2,1,0:T(1,128)S(1)} all-to-all(f32[128,1,1]{2,1,0:T(1,128)S(1)} %broadcast_in_dim.13), channel_id=1, replica_groups=mesh['tile'=128,'freq'=4] {'tile'}, dimensions={0} | all-to-all | bytes 1024 | tf_op jit(solution)/shard_map/all_to_all | solution.py:126
  101.3 0.7 reduce_sum.72
  102.7 0.5 multiply_reduce_fusion.1
  103.3 0.5 multiply_reduce_fusion.2
  103.9 3.5 %convolution_multiply_fusion = f32[16,128,32]{1,2,0:T(8,128)S(1)} fusion(f32[16,512,128]{2,1,0:T(8,128)} %shard_map.60, f32[32,512,1]{1,0,2:T(8,128)S(1)} %reshape.135, f32[16,128]{1,0:T(8,128)S(1)} %add_convert_fusion), kind=kOutput, calls=%fused_computation | convolution fusion | flops 201392128 | bytes 4530176 | tf_op jit(solution)/shard_map/vq,iqo->ivo/dot_general | solution.py:19
  107.5 0.1 broadcast_in_dim.15
  107.6 36.1 %all_to_all.38 = f32[128,16,128]{2,1,0:T(8,128)S(1)} all-to-all(f32[128,16,128]{2,1,0:T(8,128)S(1)} %bitcast.148), channel_id=1, replica_groups=mesh['tile'=128,'freq'=4] {'tile'}, dimensions={0} | all-to-all | bytes 2097152 | tf_op jit(solution)/shard_map/all_to_all | solution.py:144
  143.7 2.9 %fusion = f32[32,2,64]{2,0,1:T(8,128)S(1)} fusion(f32[32,2,64]{2,0,1:T(8,128)S(1)} %fusion.4, f32[64,32,128,1]{2,1,3,0:T(8,128)S(1)} %bitcast.151, f32[2,64,128,64]{2,1,0,3:T(8,128)S(1)} %bitcast.144), kind=kOutput, calls=%fused_computation.4 | convolution fusion | flops 201330688 | bytes 5275648 | tf_op jit(solution)/shard_map/jvo,jqo->jvq/dot_general | solution.py:19
  146.8 3.2 %fusion.12 = f32[64,128,32]{1,2,0:T(8,128)S(1)} fusion(f32[64,128,128]{2,1,0:T(8,128)} %shard_map.59, f32[32,128,1]{1,0,2:T(8,128)S(1)} %reshape.138), kind=kOutput, calls=%fused_computation.70 | convolution fusion | flops 201326592 | bytes 5259264 | tf_op jit(solution)/shard_map/vq,jqo->jvo/dot_general | solution.py:19
  150.0 37.2 %all_to_all.39 = f32[128,16,128]{2,1,0:T(8,128)S(1)} all-to-all(f32[128,16,128]{2,1,0:T(8,128)S(1)} %bitcast.147), channel_id=1, replica_groups=mesh['tile'=128,'freq'=4] {'tile'}, dimensions={0} | all-to-all | bytes 2097152 | tf_op jit(solution)/shard_map/all_to_all | solution.py:104
  187.2 0.1 reduce_sum.89
  187.3 4.1 %convolution_bitcast_fusion = f32[32,2,256]{2,0,1:T(8,128)S(1)} fusion(f32[2,256,128,16]{2,1,0,3:T(8,128)} %bitcast.146, f32[16,32,128]{2,1,0:T(8,128)S(1)} %bitcast_multiply_fusion), kind=kOutput, calls=%fused_computation.1 | convolution fusion | flops 201326592 | bytes 4521984 | tf_op jit(solution)/shard_map/ivo,iqo->ivq/dot_general | solution.py:19
  191.4 0.7 broadcast_in_dim.16
  192.2 3.4 %all-to-all-start.5 = ((f32[4,32,2,256]{3,1,2,0:T(8,128)}), f32[4,32,2,256]{3,1,2,0:T(8,128)S(1)}, u32[]{:S(2)}, u32[]{:S(2)}) async-start(f32[4,32,2,256]{3,1,2,0:T(8,128)} %broadcast_in_dim.16), calls=%async_computation.5 | async-start | bytes 524288 | tf_op jit(solution)/shard_map/all_to_all | solution.py:112
  195.7 2.4 %collective-permute-start.4 = (f32[32,2,32]{2,0,1:T(8,128)S(1)}, f32[32,2,32]{2,0,1:T(8,128)S(1)}, u32[]{:S(2)}, u32[]{:S(2)}) collective-permute-start(f32[32,2,32]{2,0,1:T(8,128)S(1)} %slice.155), channel_id=1, source_target_pairs={{0,4},{4,0},{8,12},{12,8},{16,20},{20,16},{24,28},{28,24},{32,36},... | collective-permute-start | bytes 24584 | tf_op jit(solution)/shard_map/ppermute | solution.py:77
  198.1 3.7 %all-to-all-done.5 = f32[4,32,2,256]{3,1,2,0:T(8,128)S(1)} async-done(((f32[4,32,2,256]{3,1,2,0:T(8,128)}), f32[4,32,2,256]{3,1,2,0:T(8,128)S(1)}, u32[]{:S(2)}, u32[]{:S(2)}) %all-to-all-start.5) | async-done | bytes 262176 | tf_op jit(solution)/shard_map/all_to_all | solution.py:112
  201.8 1.5 multiply_reduce_fusion
  203.3 1.3 broadcast_in_dim.17
  204.6 7.3 %all-to-all-start.6 = ((f32[128,1,1]{2,1,0:T(1,128)}), f32[128,1,1]{2,1,0:T(1,128)S(1)}, u32[]{:S(2)}, u32[]{:S(2)}) async-start(f32[128,1,1]{2,1,0:T(1,128)} %broadcast_in_dim.17), calls=%async_computation.6 | async-start | bytes 131072 | tf_op jit(solution)/shard_map/all_to_all | solution.py:126
  211.9 11.4 %all-to-all-done.6 = f32[128,1,1]{2,1,0:T(1,128)S(1)} async-done(((f32[128,1,1]{2,1,0:T(1,128)}), f32[128,1,1]{2,1,0:T(1,128)S(1)}, u32[]{:S(2)}, u32[]{:S(2)}) %all-to-all-start.6) | async-done | bytes 544 | tf_op jit(solution)/shard_map/all_to_all | solution.py:126
  223.3 0.7 reduce_sum.91
  224.8 0.1 fusion.10
  224.9 2.5 %collective-permute-start.3 = (f32[4,2,16,128]{3,2,1,0:T(8,128)S(1)}, f32[4,2,16,128]{3,2,1,0:T(8,128)S(1)}, u32[]{:S(2)}, u32[]{:S(2)}) collective-permute-start(f32[4,2,16,128]{3,2,1,0:T(8,128)S(1)} %bitcast.159), channel_id=1, source_target_pairs={{0,4},{4,0},{8,12},{12,8},{16,20},{20,16},{24,28},{28,24},{32,36},... | collective-permute-start | bytes 196616 | tf_op jit(solution)/shard_map/ppermute | solution.py:77
  227.6 0.7 reshape.131
  228.4 0.8 copy.49
  (40 shorter events, 1.3 us)
Async XLA Ops:
  0.6 37.0 %copy-start = (s32[1,16,64]{2,1,0:T(8,128)S(1)}, s32[1,16,64]{2,1,0:T(8,128)}, u32[]{:S(2)}) copy-start(s32[1,16,64]{2,1,0:T(8,128)} %param.7) | copy-start | bytes 12292
  0.6 12.5 %collective-permute-start = (f32[2,32,4096]{2,1,0:T(8,128)}, f32[2,32,4096]{2,1,0:T(8,128)S(1)}, u32[]{:S(2)}, u32[]{:S(2)}) collective-permute-start(f32[2,32,4096]{2,1,0:T(8,128)} %bitcast.153), channel_id=1, source_target_pairs={{0,4},{4,0},{8,12},{12,8},{16,20},{20,16},{24,28},{28,24},{32,36},... | collective-permute-start | bytes 3145736 | tf_op jit(solution)/shard_map/ppermute | solution.py:77
  9.4 3.3 %collective-permute-start.1 = (f32[32,128]{1,0:T(8,128)}, f32[32,128]{1,0:T(8,128)S(1)}, u32[]{:S(2)}, u32[]{:S(2)}) collective-permute-start(f32[32,128]{1,0:T(8,128)} %bitcast.160), channel_id=1, source_target_pairs={{0,4},{4,0},{8,12},{12,8},{16,20},{20,16},{24,28},{28,24},{32,36},... | collective-permute-start | bytes 49160 | tf_op jit(solution)/shard_map/ppermute | solution.py:77
  13.1 1.0 copy-start.3
  18.7 16.1 %copy-start.2 = (f32[2,1,128,1024]{3,2,1,0:T(8,128)S(1)}, f32[2,1,128,1024]{3,2,1,0:T(8,128)}, u32[]{:S(2)}) copy-start(f32[2,1,128,1024]{3,2,1,0:T(8,128)} %param.6) | copy-start | bytes 3145732
  23.1 42.6 %all-to-all-start = ((f32[128,16,128]{2,1,0:T(8,128)}), f32[128,16,128]{2,1,0:T(8,128)S(1)}, u32[]{:S(2)}, u32[]{:S(2)}) async-start(f32[128,16,128]{2,1,0:T(8,128)} %bitcast.6), calls=%async_computation | async-start | bytes 2097152 | tf_op jit(solution)/shard_map/all_to_all | solution.py:104
  34.8 5.1 %collective-permute-start.2 = (f32[2,128,1024]{2,1,0:T(8,128)S(1)}, f32[2,128,1024]{2,1,0:T(8,128)S(1)}, u32[]{:S(2)}, u32[]{:S(2)}) collective-permute-start(f32[2,128,1024]{2,1,0:T(8,128)S(1)} %bitcast.156), channel_id=1, source_target_pairs={{0,4},{4,0},{8,12},{12,8},{16,20},{20,16},{24,28},{28,24},{32,36},... | collective-permute-start | bytes 3145736 | tf_op jit(solution)/shard_map/ppermute | solution.py:77
  39.9 1.0 copy-start.4
  70.7 9.9 %all-to-all-start.1 = ((f32[4,32,2,256]{3,1,2,0:T(8,128)}), f32[4,32,2,256]{3,1,2,0:T(8,128)S(1)}, u32[]{:S(2)}, u32[]{:S(2)}) async-start(f32[4,32,2,256]{3,1,2,0:T(8,128)} %broadcast_in_dim.12), calls=%async_computation.1 | async-start | bytes 524288 | tf_op jit(solution)/shard_map/all_to_all | solution.py:112
  103.9 39.8 %copy-start.1 = (f32[64,128,128]{2,1,0:T(8,128)S(1)}, f32[64,128,128]{2,1,0:T(8,128)}, u32[]{:S(2)}) copy-start(f32[64,128,128]{2,1,0:T(8,128)} %shard_map.59) | copy-start | bytes 12582916
  192.2 9.6 %all-to-all-start.5 = ((f32[4,32,2,256]{3,1,2,0:T(8,128)}), f32[4,32,2,256]{3,1,2,0:T(8,128)S(1)}, u32[]{:S(2)}, u32[]{:S(2)}) async-start(f32[4,32,2,256]{3,1,2,0:T(8,128)} %broadcast_in_dim.16), calls=%async_computation.5 | async-start | bytes 524288 | tf_op jit(solution)/shard_map/all_to_all | solution.py:112
  195.7 16.2 %collective-permute-start.4 = (f32[32,2,32]{2,0,1:T(8,128)S(1)}, f32[32,2,32]{2,0,1:T(8,128)S(1)}, u32[]{:S(2)}, u32[]{:S(2)}) collective-permute-start(f32[32,2,32]{2,0,1:T(8,128)S(1)} %slice.155), channel_id=1, source_target_pairs={{0,4},{4,0},{8,12},{12,8},{16,20},{20,16},{24,28},{28,24},{32,36},... | collective-permute-start | bytes 24584 | tf_op jit(solution)/shard_map/ppermute | solution.py:77
  204.6 18.7 %all-to-all-start.6 = ((f32[128,1,1]{2,1,0:T(1,128)}), f32[128,1,1]{2,1,0:T(1,128)S(1)}, u32[]{:S(2)}, u32[]{:S(2)}) async-start(f32[128,1,1]{2,1,0:T(1,128)} %broadcast_in_dim.17), calls=%async_computation.6 | async-start | bytes 131072 | tf_op jit(solution)/shard_map/all_to_all | solution.py:126
  224.9 3.4 %collective-permute-start.3 = (f32[4,2,16,128]{3,2,1,0:T(8,128)S(1)}, f32[4,2,16,128]{3,2,1,0:T(8,128)S(1)}, u32[]{:S(2)}, u32[]{:S(2)}) collective-permute-start(f32[4,2,16,128]{3,2,1,0:T(8,128)S(1)} %bitcast.159), channel_id=1, source_target_pairs={{0,4},{4,0},{8,12},{12,8},{16,20},{20,16},{24,28},{28,24},{32,36},... | collective-permute-start | bytes 196616 | tf_op jit(solution)/shard_map/ppermute | solution.py:77

commit v6 on v4

--- a/solution.py
+++ b/solution.py
@@ -50,6 +50,31 @@
         out_specs=pl.BlockSpec((per_step, 4 * rows, 2 * R), lambda p: (p, 0, 0)),
         out_shape=jax.ShapeDtypeStruct((tiles, 4 * rows, 2 * R), own.dtype),
     )(own, other)
+
+def half_weight_kernel(src_ref, out_ref):
+    for jj in range(out_ref.shape[0]):
+        lo, hi = jj * R, (jj + 1) * R
+        re = src_ref[0, :, lo:hi]
+        im = src_ref[1, :, lo:hi]
+        rows = re.shape[0]
+        out_ref[jj, :rows, :R] = re
+        out_ref[jj, rows:, :R] = im
+        out_ref[jj, :rows, R:] = -im
+        out_ref[jj, rows:, R:] = re
+
+
+def build_half_weights(src):
+    rows, cols = src.shape[1], src.shape[2]
+    tiles = cols // R
+    per_step = min(tiles, 32)
+    return pl.pallas_call(
+        half_weight_kernel,
+        grid=(tiles // per_step,),
+        in_specs=[pl.BlockSpec((2, rows, per_step * R), lambda p: (0, 0, p))],
+        out_specs=pl.BlockSpec((per_step, 2 * rows, 2 * R), lambda p: (p, 0, 0)),
+        out_shape=jax.ShapeDtypeStruct((tiles, 2 * rows, 2 * R), src.dtype),
+    )(src)
+
 
 def local(observed, factor_u, factor_v, tile_ranks):
     tile_count = lax.axis_size("tile")
@@ -86,7 +111,8 @@
     obs_split = obs_both.reshape(2 * rows_u, 2, 2, half)
     target = lax.dynamic_index_in_dim(obs_split, core, axis=2, keepdims=False).transpose(2, 1, 0)
 
-    w_u = build_weights(u_own, u_other)
+    w_uo = build_half_weights(u_own)
+    w_up = build_half_weights(u_other)
     w_v = build_weights(v_own, v_other)
 
     rank_column = lax.dynamic_index_in_dim(tile_ranks[0], column, axis=1, keepdims=False)
@@ -98,8 +124,9 @@
     cos_tab, sin_tab = phases(all_freqs, all_times, total_times)
 
     def adjoint(resid):
-        lhs = resid.reshape(half, 2 * 2 * rows_u)
-        e = contract("vq,jqo->jvo", lhs, w_u)
+        lhs_o = resid[:, :, :rows_u].reshape(half, 2 * rows_u)
+        lhs_p = resid[:, :, rows_u:].reshape(half, 2 * rows_u)
+        e = contract("vq,jqo->jvo", lhs_o, w_uo) + contract("vq,jqo->jvo", lhs_p, w_up)
         outgoing = e.reshape((tile_count,) + chunk)
         incoming = lax.all_to_all(outgoing, "tile", 0, 0, tiled=True)
         gathered = incoming.reshape((row_tiles, chips_per_row_tile, 2) + chunk).sum(axis=1)
@@ -143,8 +170,9 @@
     ).reshape((tile_count,) + chunk)
     incoming = lax.all_to_all(outgoing, "tile", 0, 0, tiled=True)
     summed = incoming.reshape(col_tiles, half, 2 * R)
-    y = contract("jvo,jqo->jvq", summed, w_u).sum(axis=0)
-    residual = y.reshape(half, 2, 2 * rows_u) - target
+    y_o = contract("jvo,jqo->jvq", summed, w_uo).sum(axis=0).reshape(half, 2, rows_u)
+    y_p = contract("jvo,jqo->jvq", summed, w_up).sum(axis=0).reshape(half, 2, rows_u)
+    residual = jnp.concatenate([y_o, y_p], axis=2) - target
 
     grad2 = adjoint(residual)
     update2 = first - step_size * to_time(all_freq(grad2))

time: 229 us -> 235 us (1.026)
  blocking collectives: 92.2 us -> 101 us
  starting transfers between devices: 44.8 us -> 41.4 us
  waiting for transfers between devices: 43.4 us -> 40.1 us
    all_to_all x0 -> x1, blocking collectives: none -> 8.91 us  [all_freq(): return lax.all_to_all(outgoing, 'freq', 0, 0, tiled=True)]
    pallas_call x0 -> x2, Pallas kernels: none -> 5.48 us  [build_half_weights(): pl.pallas_call(half_weight_kernel, grid=(tiles // per_step,), in_specs=[p...]
    pallas_call x2 -> x1, Pallas kernels: 8.4 us -> 4.63 us  [build_weights(): pl.pallas_call(weight_kernel, grid=(tiles // per_step,), in_specs=[spec,...]
    all_to_all x2 -> x1, waiting for transfers between devices: 9.6 us -> 5.9 us  [all_freq(): return lax.all_to_all(outgoing, 'freq', 0, 0, tiled=True)]
    all_to_all x2 -> x1, starting transfers between devices: 7.42 us -> 4.01 us  [all_freq(): return lax.all_to_all(outgoing, 'freq', 0, 0, tiled=True)]
    dot_general x6 -> x9, matrix products: 22.3 us -> 23.6 us  [contract(): return jnp.einsum(form, left, right, precision=matmul_precision)]
  transfers between devices with their start and end apart: 9 -> 8, of which waited for: 6 -> 5; matrix products, arithmetic and copies ran while one was open for 2% -> 2% of each run, Pallas kernels for 2% -> 3%
where the time goes in v6:
time: 235 us; the launch traced here: 234 us
  blocking collectives  101 us (43%)
  starting transfers between devices  41.4 us (18%)
  waiting for transfers between devices  40.1 us (17%)
  matrix products  23.6 us (10%)
  Pallas kernels  10.1 us (4%)
  local copies, waits for them, and re-layouts  9.49 us (4%)
  other arithmetic  5.86 us (2%)
  between operations  2.51 us (1%)
    all_to_all x1, blocking collectives, adjoint(): incoming = lax.all_to_all(outgoing, 'tile', 0, 0, tiled=True)  37.2 us
    all_to_all x1, blocking collectives, local(): incoming = lax.all_to_all(outgoing, 'tile', 0, 0, tiled=True)  36.2 us
    dot_general x9, matrix products, contract(): return jnp.einsum(form, left, right, precision=matmul_precision)  23.6 us
    all_to_all x1, waiting for transfers between devices, adjoint(): incoming = lax.all_to_all(outgoing, 'tile', 0, 0, tiled=True)  20.2 us
    all_to_all x1, blocking collectives, threshold_of(): total = jnp.sum(lax.all_to_all(outgoing, 'tile', 0, 0, tiled=True))  18.9 us
    ppermute x5, starting transfers between devices, swap(): return lax.ppermute(x, 'tile', pair)  18.2 us
    all_to_all x1, starting transfers between devices, adjoint(): incoming = lax.all_to_all(outgoing, 'tile', 0, 0, tiled=True)  12.2 us
    all_to_all x1, waiting for transfers between devices, threshold_of(): total = jnp.sum(lax.all_to_all(outgoing, 'tile', 0, 0, tiled=True))  11.4 us
  transfers between devices with their start and end apart: 8, of which 5 were waited for; matrix products, arithmetic and copies ran while one was open for 2% of the time, Pallas kernels for 3%

profile of v6, /device:TPU:1, one launch (start us, length us, event | category | flops | bytes accessed | tf_op | source)
XLA Modules:
  0.0 234.3 jit_solution(8408053555615511452)
XLA Ops:
  0.6 8.8 %collective-permute-start.1 = (f32[2,32,4096]{2,1,0:T(8,128)}, f32[2,32,4096]{2,1,0:T(8,128)S(1)}, u32[]{:S(2)}, u32[]{:S(2)}) collective-permute-start(f32[2,32,4096]{2,1,0:T(8,128)} %bitcast.167), channel_id=1, source_target_pairs={{0,4},{4,0},{8,12},{12,8},{16,20},{20,16},{24,28},{28,24},{32,36},... | collective-permute-start | bytes 3145736 | tf_op jit(solution)/shard_map/ppermute | solution.py:102
  9.4 1.9 collective-permute-start
  11.4 0.8 concatenate.17
  12.2 2.8 %shard_map.59 = f32[64,64,128]{2,1,0:T(8,128)} custom-call(f32[2,32,4096]{2,1,0:T(8,128)} %bitcast.168), custom_call_target="tpu_custom_call" | custom-call | tf_op jit(solution)/shard_map/pallas_call | solution.py:70
  15.1 0.1 concatenate.18
  15.7 2.2 fusion.11
  17.9 1.0 copy-done.4
  18.9 2.7 %shard_map.60 = f32[64,64,128]{2,1,0:T(8,128)} custom-call(f32[2,32,4096]{2,1,0:T(8,128)} %copy-done.4), custom_call_target="tpu_custom_call" | custom-call | tf_op jit(solution)/shard_map/pallas_call | solution.py:70
  21.6 3.3 %convolution_add_fusion.1 = f32[32,64,128]{2,0,1:T(8,128)} fusion(f32[32,64,128]{2,0,1:T(8,128)S(1)} %fusion.11, f32[32,64,1]{1,0,2:T(8,128)S(1)} %reshape.143, f32[64,64,128]{2,1,0:T(8,128)} %shard_map.60), kind=kOutput, calls=%fused_computation.1 | convolution fusion | flops 100925440 | bytes 4202496 | tf_op jit(solution)/shard_map/vq,jqo->jvo/dot_general | solution.py:19
  25.0 12.2 %all-to-all-start = ((f32[128,16,128]{2,1,0:T(8,128)}), f32[128,16,128]{2,1,0:T(8,128)S(1)}, u32[]{:S(2)}, u32[]{:S(2)}) async-start(f32[128,16,128]{2,1,0:T(8,128)} %bitcast.7), calls=%async_computation | async-start | bytes 2097152 | tf_op jit(solution)/shard_map/all_to_all | solution.py:131
  37.1 2.8 %collective-permute-start.2 = (f32[2,128,1024]{2,1,0:T(8,128)S(1)}, f32[2,128,1024]{2,1,0:T(8,128)S(1)}, u32[]{:S(2)}, u32[]{:S(2)}) collective-permute-start(f32[2,128,1024]{2,1,0:T(8,128)S(1)} %bitcast.171), channel_id=1, source_target_pairs={{0,4},{4,0},{8,12},{12,8},{16,20},{20,16},{24,28},{28,24},{32,36},... | collective-permute-start | bytes 3145736 | tf_op jit(solution)/shard_map/ppermute | solution.py:102
  40.0 0.2 dynamic-slice_reduce_fusion
  40.3 0.1 cosine_multiply_fusion
  40.4 1.8 collective-permute-done.2.other_ref
  42.2 1.0 copy-done.6
  43.2 4.6 %shard_map.61 = f32[16,512,128]{2,1,0:T(8,128)} custom-call(f32[2,128,1024]{2,1,0:T(8,128)} %bitcast.170, f32[2,128,1024]{2,1,0:T(8,128)} %copy-done.6), custom_call_target="tpu_custom_call" | custom-call | tf_op jit(solution)/shard_map/pallas_call | solution.py:46
  47.8 20.2 %all-to-all-done = f32[128,16,128]{2,1,0:T(8,128)S(1)} async-done(((f32[128,16,128]{2,1,0:T(8,128)}), f32[128,16,128]{2,1,0:T(8,128)S(1)}, u32[]{:S(2)}, u32[]{:S(2)}) %all-to-all-start) | async-done | bytes 1048608 | tf_op jit(solution)/shard_map/all_to_all | solution.py:131
  68.2 4.1 %convolution_bitcast_fusion.1 = f32[32,2,256]{2,0,1:T(8,128)S(1)} fusion(f32[2,256,128,16]{2,1,0,3:T(8,128)} %bitcast.157, f32[16,32,128]{2,1,0:T(8,128)S(1)} %bitcast_multiply_fusion.1), kind=kOutput, calls=%fused_computation.4 | convolution fusion | flops 201326592 | bytes 4521984 | tf_op jit(solution)/shard_map/ivo,iqo->ivq/dot_general | solution.py:19
  72.3 0.8 broadcast_in_dim.12
  73.0 4.0 %all-to-all-start.1 = ((f32[4,32,2,256]{3,1,2,0:T(8,128)}), f32[4,32,2,256]{3,1,2,0:T(8,128)S(1)}, u32[]{:S(2)}, u32[]{:S(2)}) async-start(f32[4,32,2,256]{3,1,2,0:T(8,128)} %broadcast_in_dim.12), calls=%async_computation.1 | async-start | bytes 524288 | tf_op jit(solution)/shard_map/all_to_all | solution.py:139
  77.1 5.9 %all-to-all-done.1 = f32[4,32,2,256]{3,1,2,0:T(8,128)S(1)} async-done(((f32[4,32,2,256]{3,1,2,0:T(8,128)}), f32[4,32,2,256]{3,1,2,0:T(8,128)S(1)}, u32[]{:S(2)}, u32[]{:S(2)}) %all-to-all-start.1) | async-done | bytes 262176 | tf_op jit(solution)/shard_map/all_to_all | solution.py:139
  83.0 1.1 multiply_reduce_fusion.3
  84.1 0.7 broadcast_in_dim.13
  84.8 18.9 %all_to_all.37 = f32[128,1,1]{2,1,0:T(1,128)S(1)} all-to-all(f32[128,1,1]{2,1,0:T(1,128)S(1)} %broadcast_in_dim.13), channel_id=1, replica_groups=mesh['tile'=128,'freq'=4] {'tile'}, dimensions={0} | all-to-all | bytes 1024 | tf_op jit(solution)/shard_map/all_to_all | solution.py:153
  103.6 0.7 reduce_sum.72
  105.1 0.5 multiply_reduce_fusion.1
  105.6 0.5 multiply_reduce_fusion.2
  106.2 3.4 %convolution_multiply_fusion = f32[16,128,32]{1,2,0:T(8,128)S(1)} fusion(f32[16,512,128]{2,1,0:T(8,128)} %shard_map.61, f32[32,512,1]{1,0,2:T(8,128)S(1)} %reshape.146, f32[16,128]{1,0:T(8,128)S(1)} %add_convert_fusion), kind=kOutput, calls=%fused_computation.2 | convolution fusion | flops 201392128 | bytes 4530176 | tf_op jit(solution)/shard_map/vq,iqo->ivo/dot_general | solution.py:19
  109.6 0.1 broadcast_in_dim.15
  109.8 36.2 %all_to_all.38 = f32[128,16,128]{2,1,0:T(8,128)S(1)} all-to-all(f32[128,16,128]{2,1,0:T(8,128)S(1)} %bitcast.163), channel_id=1, replica_groups=mesh['tile'=128,'freq'=4] {'tile'}, dimensions={0} | all-to-all | bytes 2097152 | tf_op jit(solution)/shard_map/all_to_all | solution.py:171
  146.0 2.5 %convolution_bitcast_fusion.2 = f32[32,2,32]{2,0,1:T(8,128)S(1)} fusion(f32[64,32,128,1]{2,1,3,0:T(8,128)S(1)} %bitcast.161, f32[2,32,128,64]{2,1,0,3:T(8,128)S(1)} %bitcast.160), kind=kOutput, calls=%fused_computation.5 | convolution fusion | flops 100663296 | bytes 3153920 | tf_op jit(solution)/shard_map/jvo,jqo->jvq/dot_general | solution.py:19
  148.5 2.5 %convolution_bitcast_fusion.3 = f32[32,2,32]{2,0,1:T(8,128)S(1)} fusion(f32[64,32,128,1]{2,1,3,0:T(8,128)S(1)} %bitcast.162, f32[2,32,128,64]{2,1,0,3:T(8,128)S(1)} %bitcast.159), kind=kOutput, calls=%fused_computation.6 | convolution fusion | flops 100663296 | bytes 3153920 | tf_op jit(solution)/shard_map/jvo,jqo->jvq/dot_general | solution.py:19
  151.2 2.2 collective-permute-start.4
  153.5 0.8 collective-permute-done.4
  154.5 0.8 fusion.12
  155.2 0.8 copy-done.3
  156.0 0.8 convolution_add_fusion
  156.8 37.2 %all_to_all.39 = f32[128,16,128]{2,1,0:T(8,128)S(1)} all-to-all(f32[128,16,128]{2,1,0:T(8,128)S(1)} %bitcast.166), channel_id=1, replica_groups=mesh['tile'=128,'freq'=4] {'tile'}, dimensions={0} | all-to-all | bytes 2097152 | tf_op jit(solution)/shard_map/all_to_all | solution.py:131
  194.1 4.1 %convolution_bitcast_fusion = f32[32,2,256]{2,0,1:T(8,128)S(1)} fusion(f32[2,256,128,16]{2,1,0,3:T(8,128)} %bitcast.158, f32[16,32,128]{2,1,0:T(8,128)S(1)} %bitcast_multiply_fusion), kind=kOutput, calls=%fused_computation.3 | convolution fusion | flops 201326592 | bytes 4521984 | tf_op jit(solution)/shard_map/ivo,iqo->ivq/dot_general | solution.py:19
  198.3 8.9 %all_to_all.40 = f32[4,32,2,256]{3,1,2,0:T(8,128)S(1)} all-to-all(f32[4,32,2,256]{3,1,2,0:T(8,128)S(1)} %broadcast_in_dim.16), channel_id=1, replica_groups=mesh['tile'=128,'freq'=4] {'freq'}, dimensions={0} | all-to-all | bytes 524288 | tf_op jit(solution)/shard_map/all_to_all | solution.py:139
  207.2 1.5 multiply_reduce_fusion
  208.7 1.3 broadcast_in_dim.17
  210.0 7.0 %all-to-all-start.6 = ((f32[128,1,1]{2,1,0:T(1,128)}), f32[128,1,1]{2,1,0:T(1,128)S(1)}, u32[]{:S(2)}, u32[]{:S(2)}) async-start(f32[128,1,1]{2,1,0:T(1,128)} %broadcast_in_dim.17), calls=%async_computation.6 | async-start | bytes 131072 | tf_op jit(solution)/shard_map/all_to_all | solution.py:153
  217.0 11.4 %all-to-all-done.6 = f32[128,1,1]{2,1,0:T(1,128)S(1)} async-done(((f32[128,1,1]{2,1,0:T(1,128)}), f32[128,1,1]{2,1,0:T(1,128)S(1)}, u32[]{:S(2)}, u32[]{:S(2)}) %all-to-all-start.6) | async-done | bytes 544 | tf_op jit(solution)/shard_map/all_to_all | solution.py:153
  228.4 0.7 reduce_sum.83
  230.1 2.5 %collective-permute-start.3 = (f32[4,2,16,128]{3,2,1,0:T(8,128)S(1)}, f32[4,2,16,128]{3,2,1,0:T(8,128)S(1)}, u32[]{:S(2)}, u32[]{:S(2)}) collective-permute-start(f32[4,2,16,128]{3,2,1,0:T(8,128)S(1)} %bitcast.174), channel_id=1, source_target_pairs={{0,4},{4,0},{8,12},{12,8},{16,20},{20,16},{24,28},{28,24},{32,36},... | collective-permute-start | bytes 196616 | tf_op jit(solution)/shard_map/ppermute | solution.py:102
  232.7 0.7 reshape.141
  233.5 0.8 copy.60
  (53 shorter events, 2.0 us)
Async XLA Ops:
  0.6 39.3 %copy-start = (s32[1,16,64]{2,1,0:T(8,128)S(1)}, s32[1,16,64]{2,1,0:T(8,128)}, u32[]{:S(2)}) copy-start(s32[1,16,64]{2,1,0:T(8,128)} %param.7) | copy-start | bytes 12292
  0.6 17.3 %collective-permute-start.1 = (f32[2,32,4096]{2,1,0:T(8,128)}, f32[2,32,4096]{2,1,0:T(8,128)S(1)}, u32[]{:S(2)}, u32[]{:S(2)}) collective-permute-start(f32[2,32,4096]{2,1,0:T(8,128)} %bitcast.167), channel_id=1, source_target_pairs={{0,4},{4,0},{8,12},{12,8},{16,20},{20,16},{24,28},{28,24},{32,36},... | collective-permute-start | bytes 3145736 | tf_op jit(solution)/shard_map/ppermute | solution.py:102
  9.4 5.6 %collective-permute-start = (f32[32,128]{1,0:T(8,128)}, f32[32,128]{1,0:T(8,128)S(1)}, u32[]{:S(2)}, u32[]{:S(2)}) collective-permute-start(f32[32,128]{1,0:T(8,128)} %bitcast.175), channel_id=1, source_target_pairs={{0,4},{4,0},{8,12},{12,8},{16,20},{20,16},{24,28},{28,24},{32,36},... | collective-permute-start | bytes 49160 | tf_op jit(solution)/shard_map/ppermute | solution.py:102
  17.9 1.0 copy-start.4
  25.0 12.2 %copy-start.5 = (f32[2,1,128,1024]{3,2,1,0:T(8,128)S(1)}, f32[2,1,128,1024]{3,2,1,0:T(8,128)}, u32[]{:S(2)}) copy-start(f32[2,1,128,1024]{3,2,1,0:T(8,128)} %param.6) | copy-start | bytes 3145732
  25.0 43.1 %all-to-all-start = ((f32[128,16,128]{2,1,0:T(8,128)}), f32[128,16,128]{2,1,0:T(8,128)S(1)}, u32[]{:S(2)}, u32[]{:S(2)}) async-start(f32[128,16,128]{2,1,0:T(8,128)} %bitcast.7), calls=%async_computation | async-start | bytes 2097152 | tf_op jit(solution)/shard_map/all_to_all | solution.py:131
  37.1 5.1 %collective-permute-start.2 = (f32[2,128,1024]{2,1,0:T(8,128)S(1)}, f32[2,128,1024]{2,1,0:T(8,128)S(1)}, u32[]{:S(2)}, u32[]{:S(2)}) collective-permute-start(f32[2,128,1024]{2,1,0:T(8,128)S(1)} %bitcast.171), channel_id=1, source_target_pairs={{0,4},{4,0},{8,12},{12,8},{16,20},{20,16},{24,28},{28,24},{32,36},... | collective-permute-start | bytes 3145736 | tf_op jit(solution)/shard_map/ppermute | solution.py:102
  42.2 1.0 copy-start.6
  73.0 9.9 %all-to-all-start.1 = ((f32[4,32,2,256]{3,1,2,0:T(8,128)}), f32[4,32,2,256]{3,1,2,0:T(8,128)S(1)}, u32[]{:S(2)}, u32[]{:S(2)}) async-start(f32[4,32,2,256]{3,1,2,0:T(8,128)} %broadcast_in_dim.12), calls=%async_computation.1 | async-start | bytes 524288 | tf_op jit(solution)/shard_map/all_to_all | solution.py:139
  109.6 36.4 %copy-start.2 = (f32[64,64,128]{2,1,0:T(8,128)S(1)}, f32[64,64,128]{2,1,0:T(8,128)}, u32[]{:S(2)}) copy-start(f32[64,64,128]{2,1,0:T(8,128)} %shard_map.60) | copy-start | bytes 6291460
  146.0 2.5 %copy-start.1 = (f32[64,64,128]{2,1,0:T(8,128)S(1)}, f32[64,64,128]{2,1,0:T(8,128)}, u32[]{:S(2)}) copy-start(f32[64,64,128]{2,1,0:T(8,128)} %shard_map.59) | copy-start | bytes 6291460
  151.2 3.1 %collective-permute-start.4 = (f32[32,2,32]{2,0,1:T(8,128)S(1)}, f32[32,2,32]{2,0,1:T(8,128)S(1)}, u32[]{:S(2)}, u32[]{:S(2)}) collective-permute-start(f32[32,2,32]{2,0,1:T(8,128)S(1)} %slice.157), channel_id=1, source_target_pairs={{0,4},{4,0},{8,12},{12,8},{16,20},{20,16},{24,28},{28,24},{32,36},... | collective-permute-start | bytes 24584 | tf_op jit(solution)/shard_map/ppermute | solution.py:102
  154.5 1.6 copy-start.3
  210.0 18.4 %all-to-all-start.6 = ((f32[128,1,1]{2,1,0:T(1,128)}), f32[128,1,1]{2,1,0:T(1,128)S(1)}, u32[]{:S(2)}, u32[]{:S(2)}) async-start(f32[128,1,1]{2,1,0:T(1,128)} %broadcast_in_dim.17), calls=%async_computation.6 | async-start | bytes 131072 | tf_op jit(solution)/shard_map/all_to_all | solution.py:153
  230.1 3.4 %collective-permute-start.3 = (f32[4,2,16,128]{3,2,1,0:T(8,128)S(1)}, f32[4,2,16,128]{3,2,1,0:T(8,128)S(1)}, u32[]{:S(2)}, u32[]{:S(2)}) collective-permute-start(f32[4,2,16,128]{3,2,1,0:T(8,128)S(1)} %bitcast.174), channel_id=1, source_target_pairs={{0,4},{4,0},{8,12},{12,8},{16,20},{20,16},{24,28},{28,24},{32,36},... | collective-permute-start | bytes 196616 | tf_op jit(solution)/shard_map/ppermute | solution.py:102
